TPU v7x, 32 devices: a whole 2x2x4 slice. The times are simulated.
32 devices in a mesh: dp: 4 (over y, core), mp: 8 (over z, x).
Axes of the slice: x: 2, y: 2, z: 4, core: 2. Of those that a mesh axis runs over, the one named last changes fastest.
Arguments:
- tokens: bfloat16 [512, 6144], P('dp', 'mp'), may hold values from -6 to 6
- norm_gain: bfloat16 [6144], P('mp'), may hold values from 0.5 to 1.5
- qkv_weight: bfloat16 [3, 128, 24, 6144], P(None, 'mp', None, 'dp'), may hold values from -0.078125 to 0.078125
- head_weight: bfloat16 [128, 24, 6144], P('mp', None, 'dp'), may hold values from -0.109375 to 0.109375
- up_weight: bfloat16 [12288, 6144], P('mp', 'dp'), may hold values from -0.078125 to 0.078125
- down_weight: bfloat16 [12288, 6144], P('mp', 'dp'), may hold values from -0.0546875 to 0.0546875
- cotangent: bfloat16 [512, 6144], P('dp', 'mp'), may hold values from -6 to 6
Outputs:
- mixed: bfloat16 [512, 6144], P('dp', 'mp')
- tokens_grad: float32 [512, 6144], P('dp', 'mp')
- qkv_grad: bfloat16 [3, 128, 24, 6144], P(None, 'mp', None, 'dp')
- head_grad: bfloat16 [128, 24, 6144], P('mp', None, 'dp')
- up_grad: bfloat16 [12288, 6144], P('mp', 'dp')
- down_grad: bfloat16 [12288, 6144], P('mp', 'dp')
- gain_grad: float32 [6144], P('mp')
All inputs are finite; a program needn't handle non-finite values.
Results may differ from a plain program's by a relative error of at most 0.013.
Values may be sent and summed in bfloat16 or wider, within the bound.
No kernel may reach another device: no remote copies, remote signals or barrier semaphores. Data moves between devices by JAX's collectives and lax.ppermute only.
A program may use at most 256 MiB of HBM per device.

v0:
```python
import math

import jax
import jax.numpy as jnp
from jax import lax
from jax.sharding import PartitionSpec as P

D = 6144
HEADS = 24
HS = 128
PATCHES = 128
QB = 8
IMG_DP = 1
ROWS = 128
TQ = 16
ITEMS = 192


epsilon = 1e-06
contract_rows = (((0,), (0,)), ((), ()))
contract_cols = (((1,), (1,)), ((), ()))


def gelu_pair(inputs):
    normal_cdf = 0.5 * (1.0 + jax.scipy.special.erf(inputs * 0.7071067811865476))
    density = jnp.exp(-0.5 * inputs * inputs) * 0.3989422804014327
    return (inputs * normal_cdf, normal_cdf + inputs * density)


def head_norm(values):
    center = values - jnp.mean(values, axis=0, keepdims=True)
    inverse = lax.rsqrt(jnp.mean(center * center, axis=0, keepdims=True) + epsilon)
    return (center * inverse, inverse)


def norm_back(upstream, normed, inverse):
    return inverse * (
        upstream
        - jnp.mean(upstream, axis=0, keepdims=True)
        - normed * jnp.mean(upstream * normed, axis=0, keepdims=True)
    )


def to_items(pair_rows):
    depth = pair_rows.shape[1]
    shaped = pair_rows.reshape(2, depth, HEADS, IMG_DP, 1, PATCHES)
    spread = jnp.broadcast_to(shaped, (2, depth, HEADS, IMG_DP, QB, PATCHES))
    return jnp.transpose(spread, (1, 2, 3, 4, 0, 5)).reshape(depth, HEADS * IMG_DP * QB, 2, PATCHES)


def from_items(pair_items):
    depth = pair_items.shape[0]
    shaped = pair_items.reshape(depth, HEADS, IMG_DP, QB, 2, PATCHES)
    summed = jnp.sum(shaped.astype(jnp.float32), axis=3).astype(jnp.bfloat16)
    return jnp.transpose(summed, (3, 0, 1, 2, 4)).reshape(2, depth, HEADS, IMG_DP * PATCHES)


def attend(queries, keyvals):
    query_hat, query_scale = head_norm(queries.astype(jnp.float32))
    key_hat, key_scale = head_norm(keyvals[:, :, 0].astype(jnp.float32))
    query_norm = query_hat.astype(jnp.bfloat16)
    key_norm = key_hat.astype(jnp.bfloat16)
    factor = 1.0 / math.sqrt(queries.shape[0])
    scores = (
        jnp.einsum("cia,cib->iab", query_norm, key_norm, preferred_element_type=jnp.float32)
        * factor
    )
    raised = jnp.exp(scores)
    shares = raised / jnp.sum(raised, axis=2, keepdims=True)
    rounded = shares.astype(jnp.bfloat16)
    values = keyvals[:, :, 1]
    attended = jnp.einsum(
        "iab,cib->cia", rounded, values, preferred_element_type=jnp.float32
    ).astype(jnp.bfloat16)
    stored = (
        query_hat,
        query_scale,
        key_hat,
        key_scale,
        query_norm,
        key_norm,
        shares,
        rounded,
        values,
    )
    return (attended, stored)


def attend_back(upstream, stored):
    query_hat, query_scale, key_hat, key_scale, query_norm, key_norm, shares, rounded, values = (
        stored
    )
    factor = 1.0 / math.sqrt(upstream.shape[0])
    share_grad = jnp.einsum("cia,cib->iab", upstream, values, preferred_element_type=jnp.float32)
    value_grad = jnp.einsum("iab,cia->cib", rounded, upstream, preferred_element_type=jnp.float32)
    score_grad = (
        shares * (share_grad - jnp.sum(shares * share_grad, axis=2, keepdims=True)) * factor
    ).astype(jnp.bfloat16)
    query_back = jnp.einsum(
        "iab,cib->cia", score_grad, key_norm, preferred_element_type=jnp.float32
    )
    key_back = jnp.einsum(
        "iab,cia->cib", score_grad, query_norm, preferred_element_type=jnp.float32
    )
    query_grad = norm_back(query_back, query_hat, query_scale).astype(jnp.bfloat16)
    key_grad = norm_back(key_back, key_hat, key_scale).astype(jnp.bfloat16)
    pair_grad = jnp.stack([key_grad, value_grad.astype(jnp.bfloat16)], axis=2)
    return (query_grad, pair_grad)


def shards(tokens, norm_gain, qkv_weight, head_weight, up_weight, down_weight, cotangent):
    model_count = lax.axis_size("mp")
    head_slice = HS // model_count
    quarter = qkv_weight.shape[-1]
    rows_full, gain_row = (
        lax.all_gather(tokens, "mp", axis=1, tiled=True),
        lax.all_gather(norm_gain.reshape(1, -1), "mp", axis=1, tiled=True),
    )
    qkv_full, head_full, up_full, down_full = (
        lax.all_gather(qkv_weight.reshape(-1, quarter), "dp", axis=1, tiled=True),
        lax.all_gather(head_weight.reshape(-1, quarter), "dp", axis=1, tiled=True),
        lax.all_gather(up_weight, "dp", axis=1, tiled=True),
        lax.all_gather(down_weight, "dp", axis=1, tiled=True),
    )
    widened = rows_full.astype(jnp.float32)
    center = widened - jnp.mean(widened, axis=1, keepdims=True)
    row_scale = lax.rsqrt(jnp.mean(center * center, axis=1, keepdims=True) + epsilon)
    normed = center * row_scale
    gain_wide = gain_row.astype(jnp.float32)
    hidden_in = (normed * gain_wide).astype(jnp.bfloat16)
    projected = lax.dot_general(
        qkv_full, hidden_in, contract_cols, preferred_element_type=jnp.float32
    )
    projected = projected.astype(jnp.bfloat16).reshape(3, head_slice, HEADS, ROWS)
    queries = projected[0].reshape(head_slice, ITEMS, TQ)
    keyvals = to_items(projected[1:])
    query_heads, pair_heads = (
        lax.all_to_all(queries, "mp", split_axis=1, concat_axis=0, tiled=True),
        lax.all_to_all(keyvals, "mp", split_axis=1, concat_axis=0, tiled=True),
    )
    attended, stored = attend(query_heads, pair_heads)
    head_rows = lax.all_to_all(attended, "mp", split_axis=0, concat_axis=1, tiled=True).reshape(
        head_slice * HEADS, ROWS
    )
    up_input = lax.dot_general(
        up_full, hidden_in, contract_cols, preferred_element_type=jnp.float32
    )
    activated, gelu_slope = gelu_pair(up_input)
    up_output = activated.astype(jnp.bfloat16)
    branch = lax.dot_general(
        head_rows, head_full, contract_rows, preferred_element_type=jnp.float32
    ) + lax.dot_general(up_output, down_full, contract_rows, preferred_element_type=jnp.float32)
    branch_local = lax.psum_scatter(branch, "mp", scatter_dimension=1, tiled=True)
    mixed = (tokens.astype(jnp.float32) + branch_local).astype(jnp.bfloat16)
    cotangent_full = lax.all_gather(cotangent, "mp", axis=1, tiled=True)
    down_term = jnp.dot(up_output, cotangent_full, preferred_element_type=jnp.float32)
    head_term = jnp.dot(head_rows, cotangent_full, preferred_element_type=jnp.float32)
    up_upstream = (
        lax.dot_general(
            down_full, cotangent_full, contract_cols, preferred_element_type=jnp.float32
        )
        * gelu_slope
    ).astype(jnp.bfloat16)
    head_upstream = lax.dot_general(
        head_full, cotangent_full, contract_cols, preferred_element_type=jnp.float32
    )
    head_upstream = head_upstream.astype(jnp.bfloat16).reshape(head_slice, ITEMS, TQ)
    upstream = lax.all_to_all(head_upstream, "mp", split_axis=1, concat_axis=0, tiled=True)
    query_grad, pair_grad = attend_back(upstream, stored)
    query_local, pair_local = (
        lax.all_to_all(query_grad, "mp", split_axis=0, concat_axis=1, tiled=True),
        lax.all_to_all(pair_grad, "mp", split_axis=0, concat_axis=1, tiled=True),
    )
    proj_grad = jnp.concatenate(
        [query_local.reshape(1, head_slice, HEADS, ROWS), from_items(pair_local)], axis=0
    )
    proj_grad = proj_grad.reshape(3 * head_slice * HEADS, ROWS)
    qkv_term = jnp.dot(proj_grad, hidden_in, preferred_element_type=jnp.float32)
    up_term = jnp.dot(up_upstream, hidden_in, preferred_element_type=jnp.float32)
    input_full = lax.dot_general(
        proj_grad, qkv_full, contract_rows, preferred_element_type=jnp.float32
    ) + lax.dot_general(up_upstream, up_full, contract_rows, preferred_element_type=jnp.float32)
    input_local = lax.psum_scatter(input_full, "mp", scatter_dimension=1, tiled=True)
    shard_width = input_local.shape[1]
    normed_local = lax.dynamic_slice_in_dim(
        normed, lax.axis_index("mp") * shard_width, shard_width, 1
    )
    scaled = input_local * norm_gain.astype(jnp.float32)
    plain_sum, cross_sum = lax.psum(
        (jnp.sum(scaled, axis=1), jnp.sum(scaled * normed_local, axis=1)), "mp"
    )
    tokens_grad = row_scale * (
        scaled - plain_sum[:, None] / D - normed_local * (cross_sum[:, None] / D)
    )
    tokens_grad = tokens_grad + cotangent.astype(jnp.float32)
    gain_piece = jnp.sum(input_local * normed_local, axis=0)
    gain_grad = lax.psum(gain_piece, "dp")
    qkv_sum, head_sum, up_sum, down_sum = (
        lax.psum_scatter(
            qkv_term.astype(jnp.bfloat16), "dp", scatter_dimension=1, tiled=True
        ).astype(jnp.float32),
        lax.psum_scatter(
            head_term.astype(jnp.bfloat16), "dp", scatter_dimension=1, tiled=True
        ).astype(jnp.float32),
        lax.psum_scatter(
            up_term.astype(jnp.bfloat16), "dp", scatter_dimension=1, tiled=True
        ).astype(jnp.float32),
        lax.psum_scatter(
            down_term.astype(jnp.bfloat16), "dp", scatter_dimension=1, tiled=True
        ).astype(jnp.float32),
    )
    qkv_grad = qkv_sum.astype(jnp.bfloat16).reshape(3, head_slice, HEADS, quarter)
    head_grad = head_sum.astype(jnp.bfloat16).reshape(head_slice, HEADS, quarter)
    return (
        mixed,
        tokens_grad,
        qkv_grad,
        head_grad,
        up_sum.astype(jnp.bfloat16),
        down_sum.astype(jnp.bfloat16),
        gain_grad,
    )


def solution(mesh):
    in_specs = (
        P("dp", "mp"),
        P("mp"),
        P(None, "mp", None, "dp"),
        P("mp", None, "dp"),
        P("mp", "dp"),
        P("mp", "dp"),
        P("dp", "mp"),
    )
    out_specs = (
        P("dp", "mp"),
        P("dp", "mp"),
        P(None, "mp", None, "dp"),
        P("mp", None, "dp"),
        P("mp", "dp"),
        P("mp", "dp"),
        P("mp"),
    )
    return jax.shard_map(shards, mesh=mesh, in_specs=in_specs, out_specs=out_specs, check_vma=False)
```

profile of v0, /device:TPU:0, one launch (start us, length us, event | category | flops | bytes accessed | tf_op | source)
XLA Modules:
  0.0 1104.1 jit_solution(7017761609135249618)
XLA Ops:
  11.2 32.3 %all-gather.1 = bf16[8,1,768]{2,1,0:T(2,128)(2,1)S(1)} all-gather(bf16[1,1,768]{2,1,0:T(2,128)(2,1)S(1)} %reshape.148), channel_id=2, replica_groups=mesh['dp'=4,'mp'=8] {'mp'}, dimensions={0}, use_global_device_ids=true | all-gather | bytes 13824 | tf_op jit(solution)/shard_map/all_gather | solution.py:117
  43.6 13.8 %all-gather.9.cloned.1.call-done = bf16[128,6144]{1,0:T(8,128)(2,1)} async-done(((bf16[128,768]{1,0:T(8,128)(2,1)}), bf16[128,6144]{1,0:T(8,128)(2,1)}) %all-gather.9.cloned.1.call-update) | async-done | bytes 1572880 | tf_op jit(solution)/shard_map/all_gather | solution.py:116
  61.0 41.5 %all-gather.19.cloned.1.call-done = bf16[128,6144]{1,0:T(8,128)(2,1)} async-done(((bf16[128,768]{1,0:T(8,128)(2,1)}), bf16[128,6144]{1,0:T(8,128)(2,1)}) %all-gather.19.cloned.1.call-update) | async-done | bytes 1572880 | tf_op jit(solution)/shard_map/all_gather | solution.py:155
  102.5 37.5 %all-gather.13.cloned.1.call-done = bf16[384,6144]{1,0:T(8,128)(2,1)} async-done(((bf16[384,1536]{1,0:T(8,128)(2,1)}), bf16[384,6144]{1,0:T(8,128)(2,1)}) %all-gather.13.cloned.1.call-update) | async-done | bytes 4718608 | tf_op jit(solution)/shard_map/all_gather | solution.py:121
  140.0 4.2 convolution_convert_fusion.6
  146.8 5.5 all-to-all-start.3
  152.3 80.2 %all-gather.11.cloned.1.call-done = bf16[1152,6144]{1,0:T(8,128)(2,1)} async-done(((bf16[1152,1536]{1,0:T(8,128)(2,1)}), bf16[1152,6144]{1,0:T(8,128)(2,1)}) %all-gather.11.cloned.1.call-update) | async-done | bytes 14155792 | tf_op jit(solution)/shard_map/all_gather | solution.py:120
  232.5 9.7 fusion.5
  245.4 5.5 all-to-all-start.1
  252.3 5.8 all-to-all-done.1
  258.1 2.1 broadcast_in_dim.5
  260.2 4.8 all-to-all-start
  268.4 2.5 copy.113
  272.8 28.4 %all-to-all-done = bf16[16,192,2,128]{3,2,0,1:T(2,128)(2,1)} async-done(((bf16[16,192,2,128]{3,2,0,1:T(2,128)(2,1)}), bf16[16,192,2,128]{3,2,0,1:T(2,128)(2,1)}, u32[]{:S(2)}, u32[]{:S(2)}) %all-to-all-start) | async-done | bytes 1572896 | tf_op jit(solution)/shard_map/all_to_all | solution.py:139
  301.2 2.0 copy.108
  306.8 2.5 fusion.53
  313.2 2.3 reshape.157
  315.6 3.6 all-to-all-start.4
  319.2 3.8 bitcast_reduce_fusion
  326.2 2.2 copy.128
  328.4 6.0 all-to-all-start.5
  336.1 2.2 copy.127
  340.0 31.1 %all-to-all-done.5 = bf16[128,24,2,128]{3,1,2,0:T(8,128)(2,1)} async-done(((bf16[128,24,2,128]{3,1,2,0:T(8,128)(2,1)}), bf16[128,24,2,128]{3,1,2,0:T(8,128)(2,1)}, u32[]{:S(2)}, u32[]{:S(2)}) %all-to-all-start.5) | async-done | bytes 1572896 | tf_op jit(solution)/shard_map/all_to_all | solution.py:172
  371.1 3.5 copy.129
  374.6 2.6 reduce_sum.161
  377.3 9.0 fusion.62
  386.3 13.6 %convolution_bitcast_fusion = f32[1536,128]{0,1:T(8,128)} fusion(bf16[1536,6144]{1,0:T(8,128)(2,1)} %all-gather.15.cloned.1.call-done, f32[6144]{0:T(1024)S(1)} %bitcast.172, f32[128]{0:T(128)S(1)} %add_rsqrt_fusion.2, f32[128]{0:T(128)S(1)} %copy-done.17, bf16[128,6144]{1,0:T(8,128)(2,1)S(1)} %copy-done.1), kind=kOutput, calls=%fused_computation.14 | convolution fusion | flops 2419851264 | bytes 21259264 | tf_op jit(solution)/shard_map/dot_general | solution.py:145
  399.9 75.5 %all-gather.17.cloned.1.call-done = bf16[1536,6144]{1,0:T(8,128)(2,1)} async-done(((bf16[1536,1536]{1,0:T(8,128)(2,1)}), bf16[1536,6144]{1,0:T(8,128)(2,1)}) %all-gather.17.cloned.1.call-update) | async-done | bytes 18874384 | tf_op jit(solution)/shard_map/all_gather | solution.py:123
  475.4 14.4 %fusion.4 = bf16[1536,128]{0,1:T(8,128)(2,1)} fusion(bf16[1536,6144]{1,0:T(8,128)(2,1)} %all-gather.17.cloned.1.call-done, bf16[128,6144]{1,0:T(8,128)(2,1)} %all-gather.19.cloned.1.call-done, f32[1536,128]{0,1:T(8,128)} %convolution_bitcast_fusion), kind=kOutput, calls=%fused_computation.16 | convolution fusion | flops 2417885184 | bytes 21626880 | tf_op jit(solution)/shard_map/dot_general | solution.py:159
  489.9 5.3 convolution_add_fusion.1
  497.8 14.2 %all_to_all.90 = bf16[8,2,3072]{2,1,0:T(2,128)(2,1)S(1)} all-to-all(bf16[8,2,3072]{2,1,0:T(2,128)(2,1)S(1)} %reshape.153), channel_id=1, replica_groups=mesh['dp'=4,'mp'=8] {'mp'}, dimensions={0} | all-to-all | bytes 196608 | tf_op jit(solution)/shard_map/all_to_all | solution.py:142
  513.6 2.2 copy.118
  517.5 8.4 fusion.52
  525.9 2.7 convolution_add_fusion
  530.1 3.5 convolution_convert_fusion.3
  534.3 7.3 convolution_convert_fusion.2
  542.6 10.0 convolution_convert_fusion.1
  552.7 10.4 convolution_convert_fusion
  563.7 2.2 fusion.1
  565.9 5.4 reduce-scatter.9.cloned.1.call-done
  572.6 20.1 %all-reduce = (f32[128]{0:T(128)S(1)}, f32[128]{0:T(128)S(1)}) all-reduce(f32[128]{0:T(128)S(1)} %get-tuple-element.8, f32[128]{0:T(128)S(1)} %get-tuple-element.11), channel_id=1, replica_groups=mesh['dp'=4,'mp'=8] {'mp'}, use_global_device_ids=true, to_apply=%region_18.0 | all-reduce | flops 256 | bytes 2048 | tf_op jit(solution)/shard_map/psum | solution.py:189
  592.7 6.6 psum.23
  599.3 49.4 %reduce-scatter.7.cloned.1.call-done = f32[128,768]{1,0:T(8,128)} async-done(((f32[128,6144]{1,0:T(8,128)}), f32[128,768]{1,0:T(8,128)}) %reduce-scatter.7.cloned.1.call-update) | async-done | bytes 393232 | tf_op jit(solution)/shard_map/reduce_scatter | solution.py:153
  650.4 2.0 convert_add_fusion
  652.4 46.4 %reduce-scatter.13.cloned.1.call-done = bf16[384,1536]{1,0:T(8,128)(2,1)} async-done(((bf16[384,6144]{1,0:T(8,128)(2,1)}), bf16[384,1536]{1,0:T(8,128)(2,1)}) %reduce-scatter.13.cloned.1.call-update) | async-done | bytes 1179664 | tf_op jit(solution)/shard_map/reduce_scatter | solution.py:202
  698.8 112.7 %reduce-scatter.11.cloned.1.call-done = bf16[1152,1536]{1,0:T(8,128)(2,1)} async-done(((bf16[1152,6144]{1,0:T(8,128)(2,1)}), bf16[1152,1536]{1,0:T(8,128)(2,1)}) %reduce-scatter.11.cloned.1.call-update) | async-done | bytes 3538960 | tf_op jit(solution)/shard_map/reduce_scatter | solution.py:199
  811.5 142.9 %reduce-scatter.15.cloned.1.call-done = bf16[1536,1536]{1,0:T(8,128)(2,1)} async-done(((bf16[1536,6144]{1,0:T(8,128)(2,1)}), bf16[1536,1536]{1,0:T(8,128)(2,1)}) %reduce-scatter.15.cloned.1.call-update) | async-done | bytes 4718608 | tf_op jit(solution)/shard_map/reduce_scatter | solution.py:205
  954.4 142.4 %reduce-scatter.17.cloned.1.call-done = bf16[1536,1536]{1,0:T(8,128)(2,1)} async-done(((bf16[1536,6144]{1,0:T(8,128)(2,1)}), bf16[1536,1536]{1,0:T(8,128)(2,1)}) %reduce-scatter.17.cloned.1.call-update) | async-done | bytes 4718608 | tf_op jit(solution)/shard_map/reduce_scatter | solution.py:208
  (135 shorter events, 46.9 us)
Async XLA Ops:
  7.2 50.2 %all-gather.9.cloned.1.call-start = ((), (), s32[]{:S(2)}) async-start(), calls=%async_computation.12 | async-start | bytes 1769472 | tf_op jit(solution)/shard_map/all_gather | solution.py:116
  7.9 94.6 %all-gather.19.cloned.1.call-start = ((), (), s32[]{:S(2)}) async-start(), calls=%async_computation.18 | async-start | bytes 1769472 | tf_op jit(solution)/shard_map/all_gather | solution.py:155
  8.6 131.4 %all-gather.13.cloned.1.call-start = ((), (), s32[]{:S(2)}) async-start(), calls=%async_computation.14 | async-start | bytes 5898240 | tf_op jit(solution)/shard_map/all_gather | solution.py:121
  9.4 223.1 %all-gather.11.cloned.1.call-start = ((), (), s32[]{:S(2)}) async-start(), calls=%async_computation.13 | async-start | bytes 17694720 | tf_op jit(solution)/shard_map/all_gather | solution.py:120
  10.0 376.3 %all-gather.15.cloned.1.call-start = ((), (), s32[]{:S(2)}) async-start(), calls=%async_computation.15 | async-start | bytes 23592960 | tf_op jit(solution)/shard_map/all_gather | solution.py:122
  10.5 0.7 copy-start.18
  10.6 464.9 %all-gather.17.cloned.1.call-start = ((), (), s32[]{:S(2)}) async-start(), calls=%async_computation.16 | async-start | bytes 23592960 | tf_op jit(solution)/shard_map/all_gather | solution.py:123
  43.6 188.9 %copy-start.8 = (f32[8,1,768]{2,1,0:T(1,128)}, f32[8,1,768]{2,1,0:T(1,128)S(1)}, u32[]{:S(2)}) copy-start(f32[8,1,768]{2,1,0:T(1,128)S(1)} %mul.210) | copy-start | bytes 73732
  59.0 173.5 %copy-start.16 = (f32[128]{0:T(128)}, f32[128]{0:T(128)S(1)}, u32[]{:S(2)}) copy-start(f32[128]{0:T(128)S(1)} %broadcast_multiply_fusion.8) | copy-start | bytes 1540
  144.2 88.3 %copy-start.1 = (bf16[128,6144]{1,0:T(8,128)(2,1)S(1)}, bf16[128,6144]{1,0:T(8,128)(2,1)}, u32[]{:S(2)}) copy-start(bf16[128,6144]{1,0:T(8,128)(2,1)} %all-gather.9.cloned.1.call-done) | copy-start | bytes 4718596
  146.8 98.7 %all-to-all-start.3 = ((bf16[8,2,3072]{2,1,0:T(2,128)(2,1)}), bf16[8,2,3072]{2,1,0:T(2,128)(2,1)S(1)}, u32[]{:S(2)}, u32[]{:S(2)}) async-start(bf16[8,2,3072]{2,1,0:T(2,128)(2,1)} %reshape.155), calls=%async_computation.4 | async-start | bytes 196608 | tf_op jit(solution)/shard_map/all_to_all | solution.py:168
  242.2 0.7 copy-start.11
  245.4 12.6 %all-to-all-start.1 = ((bf16[8,2,3072]{2,1,0:T(2,128)(2,1)}), bf16[8,2,3072]{2,1,0:T(2,128)(2,1)S(1)}, u32[]{:S(2)}, u32[]{:S(2)}) async-start(bf16[8,2,3072]{2,1,0:T(2,128)(2,1)} %reshape.151), calls=%async_computation.1 | async-start | bytes 196608 | tf_op jit(solution)/shard_map/all_to_all | solution.py:138
  260.2 41.0 %all-to-all-start = ((bf16[16,192,2,128]{3,2,0,1:T(2,128)(2,1)}), bf16[16,192,2,128]{3,2,0,1:T(2,128)(2,1)}, u32[]{:S(2)}, u32[]{:S(2)}) async-start(bf16[16,192,2,128]{3,2,0,1:T(2,128)(2,1)} %bitcast.5), calls=%async_computation | async-start | bytes 3145728 | tf_op jit(solution)/shard_map/all_to_all | solution.py:139
  268.2 38.6 %copy-start.14 = (f32[24,16]{1,0:T(8,128)}, f32[24,16]{1,0:T(8,128)S(1)}, u32[]{:S(2)}) copy-start(f32[24,16]{1,0:T(8,128)S(1)} %copy.114) | copy-start | bytes 4612
  268.4 38.4 %copy-start.15 = (f32[24,16]{1,0:T(8,128)}, f32[24,16]{1,0:T(8,128)S(1)}, u32[]{:S(2)}) copy-start(f32[24,16]{1,0:T(8,128)S(1)} %copy.115) | copy-start | bytes 4612
  304.6 6.1 copy-start.13
  315.6 12.8 %all-to-all-start.4 = ((bf16[8,2,3072]{2,1,0:T(2,128)(2,1)}), bf16[8,2,3072]{2,1,0:T(2,128)(2,1)S(1)}, u32[]{:S(2)}, u32[]{:S(2)}) async-start(bf16[8,2,3072]{2,1,0:T(2,128)(2,1)} %reshape.157), calls=%async_computation.5 | async-start | bytes 196608 | tf_op jit(solution)/shard_map/all_to_all | solution.py:171
  323.0 2.7 copy-start.12
  328.4 42.7 %all-to-all-start.5 = ((bf16[128,24,2,128]{3,1,2,0:T(8,128)(2,1)}), bf16[128,24,2,128]{3,1,2,0:T(8,128)(2,1)}, u32[]{:S(2)}, u32[]{:S(2)}) async-start(bf16[128,24,2,128]{3,1,2,0:T(8,128)(2,1)} %copy.128), calls=%async_computation.6 | async-start | bytes 3145728 | tf_op jit(solution)/shard_map/all_to_all | solution.py:172
  334.4 236.9 %reduce-scatter.9.cloned.1.call-start = ((), (), s32[]{:S(2)}) async-start(), calls=%async_computation.19 | async-start | bytes 3538944 | tf_op jit(solution)/shard_map/reduce_scatter | solution.py:183
  377.3 9.0 copy-start.9
  377.3 9.0 copy-start.17
  475.4 14.4 %copy-start = (bf16[1536,6144]{1,0:T(8,128)(2,1)S(1)}, bf16[1536,6144]{1,0:T(8,128)(2,1)}, u32[]{:S(2)}) copy-start(bf16[1536,6144]{1,0:T(8,128)(2,1)} %all-gather.15.cloned.1.call-done) | copy-start | bytes 56623108
  475.4 14.4 %copy-start.3 = (f32[128,6144]{1,0:T(8,128)S(1)}, f32[128,6144]{1,0:T(8,128)}, u32[]{:S(2)}) copy-start(f32[128,6144]{1,0:T(8,128)} %fusion.62) | copy-start | bytes 9437188
  495.2 153.5 %reduce-scatter.7.cloned.1.call-start = ((), (), s32[]{:S(2)}) async-start(), calls=%async_computation.17 | async-start | bytes 3538944 | tf_op jit(solution)/shard_map/reduce_scatter | solution.py:153
  496.7 20.8 %copy-start.4 = (f32[1536,128]{0,1:T(8,128)S(1)}, f32[1536,128]{0,1:T(8,128)}, u32[]{:S(2)}) copy-start(f32[1536,128]{0,1:T(8,128)} %convolution_bitcast_fusion) | copy-start | bytes 2359300
  512.0 13.9 %slice-start = ((s8[4718592]{0:T(1024)(128)(4,1)}), s8[524288]{0:T(1024)(128)(4,1)S(1)}, s32[]{:S(2)}) async-start(s8[4718592]{0:T(1024)(128)(4,1)} %bitcast.141), calls=%async_computation.24 | async-start | bytes 1048576
  517.5 8.4 slice-start.1
  528.6 1.4 copy-start.2
  528.7 170.1 %reduce-scatter.13.cloned.1.call-start = ((), (), s32[]{:S(2)}) async-start(), calls=%async_computation.21 | async-start | bytes 5898240 | tf_op jit(solution)/shard_map/reduce_scatter | solution.py:202
  533.6 0.7 copy-start.10
  533.6 277.9 %reduce-scatter.11.cloned.1.call-start = ((), (), s32[]{:S(2)}) async-start(), calls=%async_computation.20 | async-start | bytes 17694720 | tf_op jit(solution)/shard_map/reduce_scatter | solution.py:199
  541.6 1.0 copy-start.5
  541.6 412.8 %reduce-scatter.15.cloned.1.call-start = ((), (), s32[]{:S(2)}) async-start(), calls=%async_computation.22 | async-start | bytes 23592960 | tf_op jit(solution)/shard_map/reduce_scatter | solution.py:205
  552.6 544.2 %reduce-scatter.17.cloned.1.call-start = ((), (), s32[]{:S(2)}) async-start(), calls=%async_computation.23 | async-start | bytes 23592960 | tf_op jit(solution)/shard_map/reduce_scatter | solution.py:208
  563.0 0.7 copy-start.19
  563.1 85.6 %copy-start.6 = (bf16[128,768]{1,0:T(8,128)(2,1)S(1)}, bf16[128,768]{1,0:T(8,128)(2,1)}, u32[]{:S(2)}) copy-start(bf16[128,768]{1,0:T(8,128)(2,1)} %param.7) | copy-start | bytes 589828
  563.7 86.7 %copy-start.7 = (bf16[128,768]{1,0:T(8,128)(2,1)S(1)}, bf16[128,768]{1,0:T(8,128)(2,1)}, u32[]{:S(2)}) copy-start(bf16[128,768]{1,0:T(8,128)(2,1)} %param.13) | copy-start | bytes 589828
Sparse Core Ops, SparseCore 0:
  10.2 47.0 all-gather.8
  59.5 42.9 all-gather.18
  104.1 35.9 all-gather.12
  141.4 91.0 all-gather.10
  233.9 119.9 all-gather.14
  355.4 119.9 all-gather.16
  495.3 75.9 reduce-scatter.8
  574.9 73.7 reduce-scatter.6
  651.8 46.9 reduce-scatter.12
  702.0 109.4 reduce-scatter.10
  814.9 139.4 reduce-scatter.14
  957.4 139.3 reduce-scatter.16
where the time goes:
time: 1110 us; the launch traced here: 1100 us
  waiting for transfers between devices  817 us (74%)
  matrix products  109 us (10%)
  blocking collectives  73.2 us (7%)
  local copies, waits for them, and re-layouts  45.8 us (4%)
  starting transfers between devices  26.3 us (2%)
  other arithmetic  18.2 us (2%)
  between operations  15.1 us (1%)
    reduce_scatter x1, waiting for transfers between devices, shards(): lax.psum_scatter(up_term.astype(jnp.bfloat16), 'dp', scatter_dimension=1,...  143 us
    reduce_scatter x1, waiting for transfers between devices, shards(): lax.psum_scatter(down_term.astype(jnp.bfloat16), 'dp', scatter_dimension=...  142 us
    reduce_scatter x1, waiting for transfers between devices, shards(): lax.psum_scatter(qkv_term.astype(jnp.bfloat16), 'dp', scatter_dimension=1...  113 us
    all_gather x1, waiting for transfers between devices, shards(): lax.all_gather(qkv_weight.reshape(-1, quarter), 'dp', axis=1, tiled=True)  80.2 us
    all_gather x1, waiting for transfers between devices, shards(): lax.all_gather(down_weight, 'dp', axis=1, tiled=True)  75.5 us
    reduce_scatter x1, waiting for transfers between devices, shards(): lax.psum_scatter(branch, 'mp', scatter_dimension=1, tiled=True)  49.4 us
    reduce_scatter x1, waiting for transfers between devices, shards(): lax.psum_scatter(head_term.astype(jnp.bfloat16), 'dp', scatter_dimension=...  46.4 us
    all_gather x1, waiting for transfers between devices, shards(): cotangent_full = lax.all_gather(cotangent, 'mp', axis=1, tiled=True)  41.5 us
  transfers between devices with their start and end apart: 17, of which 14 were waited for; matrix products, arithmetic and copies ran while one was open for 13% of the time, Pallas kernels for 0%

commit v1 on v0

--- a/solution.py
+++ b/solution.py
@@ -108,30 +108,88 @@
     return (query_grad, pair_grad)
 
 
+def swap_pairs(n_dp, n_mp):
+    ratio = n_mp // n_dp
+    pairs = []
+    for row in range(n_dp):
+        for col in range(n_mp):
+            owner, part = divmod(col, ratio)
+            pairs.append((row * n_mp + col, owner * n_mp + row * ratio + part))
+    return pairs
+
+
+def swap(block):
+    n_dp, n_mp = lax.axis_size("dp"), lax.axis_size("mp")
+    return lax.ppermute(block, ("dp", "mp"), swap_pairs(n_dp, n_mp))
+
+
+def spread_quarter(block):
+    n_dp, n_mp = lax.axis_size("dp"), lax.axis_size("mp")
+    ratio = n_mp // n_dp
+    rows, width = block.shape
+    pieces = lax.all_gather(swap(block), "mp", axis=0, tiled=False)
+    pieces = pieces.reshape(n_dp, ratio, rows, width)
+    return jnp.transpose(pieces, (0, 2, 1, 3)).reshape(n_dp * rows, ratio * width)
+
+
+def gather_quarter(partial, rows):
+    n_dp, n_mp = lax.axis_size("dp"), lax.axis_size("mp")
+    ratio = n_mp // n_dp
+    width = partial.shape[1] // ratio
+    pieces = partial.reshape(n_dp, rows, ratio, width)
+    pieces = jnp.transpose(pieces, (0, 2, 1, 3)).reshape(n_mp, rows, width)
+    summed = lax.psum_scatter(pieces, "mp", scatter_dimension=0, tiled=True)
+    return swap(summed.reshape(rows, width))
+
+
+def blockwise_grad(left, right, n_blocks):
+    rows = left.shape[1] // n_blocks
+    total = None
+    for block in range(n_blocks):
+        piece = jnp.dot(
+            left[:, block * rows:(block + 1) * rows],
+            right[block * rows:(block + 1) * rows],
+            preferred_element_type=jnp.float32,
+        ).astype(jnp.bfloat16).astype(jnp.float32)
+        total = piece if total is None else total + piece
+    return total.astype(jnp.bfloat16)
+
+
 def shards(tokens, norm_gain, qkv_weight, head_weight, up_weight, down_weight, cotangent):
-    model_count = lax.axis_size("mp")
-    head_slice = HS // model_count
+    n_dp, n_mp = lax.axis_size("dp"), lax.axis_size("mp")
+    head_slice = HS // n_mp
     quarter = qkv_weight.shape[-1]
-    rows_full, gain_row = (
-        lax.all_gather(tokens, "mp", axis=1, tiled=True),
-        lax.all_gather(norm_gain.reshape(1, -1), "mp", axis=1, tiled=True),
-    )
-    qkv_full, head_full, up_full, down_full = (
-        lax.all_gather(qkv_weight.reshape(-1, quarter), "dp", axis=1, tiled=True),
-        lax.all_gather(head_weight.reshape(-1, quarter), "dp", axis=1, tiled=True),
-        lax.all_gather(up_weight, "dp", axis=1, tiled=True),
-        lax.all_gather(down_weight, "dp", axis=1, tiled=True),
-    )
-    widened = rows_full.astype(jnp.float32)
-    center = widened - jnp.mean(widened, axis=1, keepdims=True)
-    row_scale = lax.rsqrt(jnp.mean(center * center, axis=1, keepdims=True) + epsilon)
-    normed = center * row_scale
-    gain_wide = gain_row.astype(jnp.float32)
-    hidden_in = (normed * gain_wide).astype(jnp.bfloat16)
+    rows, width = tokens.shape
+    qkv_flat = qkv_weight.reshape(-1, quarter)
+    head_flat = head_weight.reshape(-1, quarter)
+
+    widened = tokens.astype(jnp.float32)
+    block_mean = jnp.mean(widened, axis=1)
+    block_center = widened - block_mean[:, None]
+    block_m2 = jnp.sum(block_center * block_center, axis=1)
+    stats = lax.all_gather(jnp.stack([block_mean, block_m2]), "mp", axis=0, tiled=False)
+    row_mean = jnp.mean(stats[:, 0], axis=0)
+    spread = stats[:, 0] - row_mean[None, :]
+    row_m2 = jnp.sum(stats[:, 1], axis=0) + width * jnp.sum(spread * spread, axis=0)
+    row_scale = lax.rsqrt(row_m2 / D + epsilon)[:, None]
+    normed = (widened - row_mean[:, None]) * row_scale
+    gain_wide = norm_gain.astype(jnp.float32)
+    hidden_local = (normed * gain_wide).astype(jnp.bfloat16)
+    hidden_all = spread_quarter(hidden_local)
+    cot_all = spread_quarter(cotangent)
+
     projected = lax.dot_general(
-        qkv_full, hidden_in, contract_cols, preferred_element_type=jnp.float32
-    )
+        qkv_flat, hidden_all, contract_cols, preferred_element_type=jnp.float32
+    )
+    projected = lax.psum_scatter(projected, "dp", scatter_dimension=1, tiled=True)
     projected = projected.astype(jnp.bfloat16).reshape(3, head_slice, HEADS, ROWS)
+    up_input = lax.dot_general(
+        up_weight, hidden_all, contract_cols, preferred_element_type=jnp.float32
+    )
+    up_input = lax.psum_scatter(up_input, "dp", scatter_dimension=1, tiled=True)
+    activated, gelu_slope = gelu_pair(up_input)
+    up_output = activated.astype(jnp.bfloat16)
+
     queries = projected[0].reshape(head_slice, ITEMS, TQ)
     keyvals = to_items(projected[1:])
     query_heads, pair_heads = (
@@ -142,28 +200,25 @@
     head_rows = lax.all_to_all(attended, "mp", split_axis=0, concat_axis=1, tiled=True).reshape(
         head_slice * HEADS, ROWS
     )
-    up_input = lax.dot_general(
-        up_full, hidden_in, contract_cols, preferred_element_type=jnp.float32
-    )
-    activated, gelu_slope = gelu_pair(up_input)
-    up_output = activated.astype(jnp.bfloat16)
+    head_rows_all = lax.all_gather(head_rows, "dp", axis=1, tiled=True)
+    up_output_all = lax.all_gather(up_output, "dp", axis=1, tiled=True)
     branch = lax.dot_general(
-        head_rows, head_full, contract_rows, preferred_element_type=jnp.float32
-    ) + lax.dot_general(up_output, down_full, contract_rows, preferred_element_type=jnp.float32)
-    branch_local = lax.psum_scatter(branch, "mp", scatter_dimension=1, tiled=True)
-    mixed = (tokens.astype(jnp.float32) + branch_local).astype(jnp.bfloat16)
-    cotangent_full = lax.all_gather(cotangent, "mp", axis=1, tiled=True)
-    down_term = jnp.dot(up_output, cotangent_full, preferred_element_type=jnp.float32)
-    head_term = jnp.dot(head_rows, cotangent_full, preferred_element_type=jnp.float32)
-    up_upstream = (
-        lax.dot_general(
-            down_full, cotangent_full, contract_cols, preferred_element_type=jnp.float32
-        )
-        * gelu_slope
-    ).astype(jnp.bfloat16)
+        head_rows_all, head_flat, contract_rows, preferred_element_type=jnp.float32
+    ) + lax.dot_general(up_output_all, down_weight, contract_rows, preferred_element_type=jnp.float32)
+    branch_local = gather_quarter(branch, rows)
+    mixed = (widened + branch_local).astype(jnp.bfloat16)
+
+    down_grad = blockwise_grad(up_output_all, cot_all, n_dp)
+    head_grad = blockwise_grad(head_rows_all, cot_all, n_dp)
+    up_back = lax.dot_general(
+        down_weight, cot_all, contract_cols, preferred_element_type=jnp.float32
+    )
+    up_back = lax.psum_scatter(up_back, "dp", scatter_dimension=1, tiled=True)
+    up_upstream = (up_back * gelu_slope).astype(jnp.bfloat16)
     head_upstream = lax.dot_general(
-        head_full, cotangent_full, contract_cols, preferred_element_type=jnp.float32
-    )
+        head_flat, cot_all, contract_cols, preferred_element_type=jnp.float32
+    )
+    head_upstream = lax.psum_scatter(head_upstream, "dp", scatter_dimension=1, tiled=True)
     head_upstream = head_upstream.astype(jnp.bfloat16).reshape(head_slice, ITEMS, TQ)
     upstream = lax.all_to_all(head_upstream, "mp", split_axis=1, concat_axis=0, tiled=True)
     query_grad, pair_grad = attend_back(upstream, stored)
@@ -175,49 +230,32 @@
         [query_local.reshape(1, head_slice, HEADS, ROWS), from_items(pair_local)], axis=0
     )
     proj_grad = proj_grad.reshape(3 * head_slice * HEADS, ROWS)
-    qkv_term = jnp.dot(proj_grad, hidden_in, preferred_element_type=jnp.float32)
-    up_term = jnp.dot(up_upstream, hidden_in, preferred_element_type=jnp.float32)
-    input_full = lax.dot_general(
-        proj_grad, qkv_full, contract_rows, preferred_element_type=jnp.float32
-    ) + lax.dot_general(up_upstream, up_full, contract_rows, preferred_element_type=jnp.float32)
-    input_local = lax.psum_scatter(input_full, "mp", scatter_dimension=1, tiled=True)
-    shard_width = input_local.shape[1]
-    normed_local = lax.dynamic_slice_in_dim(
-        normed, lax.axis_index("mp") * shard_width, shard_width, 1
-    )
-    scaled = input_local * norm_gain.astype(jnp.float32)
+    proj_grad_all = lax.all_gather(proj_grad, "dp", axis=1, tiled=True)
+    up_upstream_all = lax.all_gather(up_upstream, "dp", axis=1, tiled=True)
+    qkv_grad = blockwise_grad(proj_grad_all, hidden_all, n_dp)
+    up_grad = blockwise_grad(up_upstream_all, hidden_all, n_dp)
+    input_partial = lax.dot_general(
+        proj_grad_all, qkv_flat, contract_rows, preferred_element_type=jnp.float32
+    ) + lax.dot_general(up_upstream_all, up_weight, contract_rows, preferred_element_type=jnp.float32)
+    input_local = gather_quarter(input_partial, rows)
+
+    scaled = input_local * gain_wide
     plain_sum, cross_sum = lax.psum(
-        (jnp.sum(scaled, axis=1), jnp.sum(scaled * normed_local, axis=1)), "mp"
+        (jnp.sum(scaled, axis=1), jnp.sum(scaled * normed, axis=1)), "mp"
     )
     tokens_grad = row_scale * (
-        scaled - plain_sum[:, None] / D - normed_local * (cross_sum[:, None] / D)
+        scaled - plain_sum[:, None] / D - normed * (cross_sum[:, None] / D)
     )
     tokens_grad = tokens_grad + cotangent.astype(jnp.float32)
-    gain_piece = jnp.sum(input_local * normed_local, axis=0)
+    gain_piece = jnp.sum(input_local * normed, axis=0)
     gain_grad = lax.psum(gain_piece, "dp")
-    qkv_sum, head_sum, up_sum, down_sum = (
-        lax.psum_scatter(
-            qkv_term.astype(jnp.bfloat16), "dp", scatter_dimension=1, tiled=True
-        ).astype(jnp.float32),
-        lax.psum_scatter(
-            head_term.astype(jnp.bfloat16), "dp", scatter_dimension=1, tiled=True
-        ).astype(jnp.float32),
-        lax.psum_scatter(
-            up_term.astype(jnp.bfloat16), "dp", scatter_dimension=1, tiled=True
-        ).astype(jnp.float32),
-        lax.psum_scatter(
-            down_term.astype(jnp.bfloat16), "dp", scatter_dimension=1, tiled=True
-        ).astype(jnp.float32),
-    )
-    qkv_grad = qkv_sum.astype(jnp.bfloat16).reshape(3, head_slice, HEADS, quarter)
-    head_grad = head_sum.astype(jnp.bfloat16).reshape(head_slice, HEADS, quarter)
     return (
         mixed,
         tokens_grad,
-        qkv_grad,
-        head_grad,
-        up_sum.astype(jnp.bfloat16),
-        down_sum.astype(jnp.bfloat16),
+        qkv_grad.reshape(qkv_weight.shape),
+        head_grad.reshape(head_weight.shape),
+        up_grad,
+        down_grad,
         gain_grad,
     )
 

time: 1110 us -> 616 us (0.55)
  waiting for transfers between devices: 817 us -> 242 us
  local copies, waits for them, and re-layouts: 45.8 us -> 110 us
  starting transfers between devices: 26.3 us -> 45.8 us
  other arithmetic: 18.2 us -> 29.7 us
  matrix products: 109 us -> 97.6 us
    reduce_scatter x6, waiting for transfers between devices: 499 us -> 111 us  [the longest x2 79.7 us: gather_quarter(): summed = lax.psum_scatter(pieces, 'mp', scatter_dimension=0, tiled=True)]
    all_gather x6 -> x5, waiting for transfers between devices: 249 us -> 90.2 us  [the longest x2 61.4 us: spread_quarter(): pieces = lax.all_gather(swap(block), 'mp', axis=0, tiled=False)]
    all_to_all x1, waiting for transfers between devices: 28.4 us -> 3.89 us  [shards(): lax.all_to_all(keyvals, 'mp', split_axis=1, concat_axis=0, tiled=True)]
    all_to_all x1 -> x0, blocking collectives: 14.2 us -> none  [shards(): lax.all_to_all(attended, 'mp', split_axis=0, concat_axis=1, tiled=True)]
    ppermute x0 -> x4, starting transfers between devices: none -> 13.8 us  [swap(): return lax.ppermute(block, ('dp', 'mp'), swap_pairs(n_dp, n_mp))]
    dot_general x12 -> x24, matrix products: 98.5 us -> 84.8 us  [the longest x16 43.7 us: blockwise_grad(): jnp.dot(left[:, block * rows:(block + 1) * rows], right[block * rows:(blo...]
    unnamed x53 -> x86, local copies, waits for them, and re-layouts: 14.1 us -> 24.5 us
    all_gather x1 -> x2, blocking collectives: 32.3 us -> 37.3 us  [the longest x1 31 us: shards(): lax.all_gather(jnp.stack([block_mean, block_m2]), 'mp', axis=0, tiled=False)]
  transfers between devices with their start and end apart: 17 -> 21, of which waited for: 14 -> 12; matrix products, arithmetic and copies ran while one was open for 13% -> 37% of each run, Pallas kernels for 0% -> 0%
where the time goes in v1:
time: 616 us; the launch traced here: 605 us
  waiting for transfers between devices  242 us (39%)
  local copies, waits for them, and re-layouts  110 us (18%)
  matrix products  97.6 us (16%)
  blocking collectives  65 us (11%)
  starting transfers between devices  45.8 us (7%)
  other arithmetic  29.7 us (5%)
  between operations  14.9 us (2%)
    reduce_scatter x2, waiting for transfers between devices, gather_quarter(): summed = lax.psum_scatter(pieces, 'mp', scatter_dimension=0, tiled=True)  79.7 us
    all_gather x2, waiting for transfers between devices, spread_quarter(): pieces = lax.all_gather(swap(block), 'mp', axis=0, tiled=False)  61.4 us
    dot_general x16, matrix products, blockwise_grad(): jnp.dot(left[:, block * rows:(block + 1) * rows], right[block * rows:(blo...  43.7 us
    all_gather x1, blocking collectives, shards(): lax.all_gather(jnp.stack([block_mean, block_m2]), 'mp', axis=0, tiled=False)  31 us
    all_to_all x1, waiting for transfers between devices, shards(): lax.all_to_all(pair_grad, 'mp', split_axis=0, concat_axis=1, tiled=True)  29.3 us
    unnamed x86, local copies, waits for them, and re-layouts  24.5 us
    reduce_scatter x1, waiting for transfers between devices, shards(): lax.psum_scatter(projected, 'dp', scatter_dimension=1, tiled=True)  21.7 us
    psum x1, blocking collectives, shards(): lax.psum((jnp.sum(scaled, axis=1), jnp.sum(scaled * normed, axis=1)), 'mp')  20.9 us
  transfers between devices with their start and end apart: 21, of which 12 were waited for; matrix products, arithmetic and copies ran while one was open for 37% of the time, Pallas kernels for 0%

profile of v1, /device:TPU:0, one launch (start us, length us, event | category | flops | bytes accessed | tf_op | source)
XLA Modules:
  0.0 604.6 jit_solution(15431614046644285964)
XLA Ops:
  7.2 3.4 collective-permute-start.2
  13.6 31.0 %all-gather.3 = f32[8,2,128]{2,1,0:T(2,128)S(1)} all-gather(f32[1,2,128]{2,1,0:T(2,128)S(1)} %maximum_bitcast_fusion), channel_id=2, replica_groups=mesh['dp'=4,'mp'=8] {'mp'}, dimensions={0}, use_global_device_ids=true | all-gather | bytes 9216 | tf_op jit(solution)/shard_map/all_gather | solution.py:170
  47.1 21.2 %all-gather.18.cloned.1.call-done = bf16[1024,768]{1,0:T(8,128)(2,1)} async-done(((bf16[128,768]{1,0:T(8,128)(2,1)}), bf16[1024,768]{1,0:T(8,128)(2,1)}) %all-gather.18.cloned.1.call-update) | async-done | bytes 1572880 | tf_op jit(solution)/shard_map/all_gather | solution.py:130
  68.4 3.0 copy.187
  74.6 40.2 %all-gather.16.cloned.1.call-done = bf16[1024,768]{1,0:T(8,128)(2,1)} async-done(((bf16[128,768]{1,0:T(8,128)(2,1)}), bf16[1024,768]{1,0:T(8,128)(2,1)}) %all-gather.16.cloned.1.call-update) | async-done | bytes 1572880 | tf_op jit(solution)/shard_map/all_gather | solution.py:130
  114.8 3.0 copy.172
  119.3 3.6 convolution_bitcast_fusion.1
  123.0 7.3 %fusion.110 = f32[1536,512]{0,1:T(8,128)} fusion(bf16[1536,1536]{1,0:T(8,128)(2,1)} %param.12, bf16[512,1536]{1,0:T(8,128)(2,1)} %bitcast.239), kind=kOutput, calls=%fused_computation.162 | convolution fusion | flops 2415919104 | bytes 9437184 | tf_op jit(solution)/shard_map/dot_general | solution.py:213
  130.3 9.7 %reduce-scatter.13.cloned.1.call-done = f32[384,128]{1,0:T(8,128)} async-done(((f32[384,512]{1,0:T(8,128)}), f32[384,128]{1,0:T(8,128)}) %reduce-scatter.13.cloned.1.call-update) | async-done | bytes 196624 | tf_op jit(solution)/shard_map/reduce_scatter | solution.py:221
  149.0 5.5 all-to-all-start.3
  154.5 21.7 %reduce-scatter.7.cloned.1.call-done = f32[1152,128]{0,1:T(8,128)} async-done(((f32[1152,512]{0,1:T(8,128)}), f32[1152,128]{0,1:T(8,128)}) %reduce-scatter.7.cloned.1.call-update) | async-done | bytes 589840 | tf_op jit(solution)/shard_map/reduce_scatter | solution.py:184
  187.8 5.7 all-to-all-start.1
  200.7 3.0 broadcast_in_dim.5
  203.7 4.3 all-to-all-start
  208.1 7.2 %convolution_bitcast_fusion = f32[1536,512]{0,1:T(8,128)} fusion(bf16[512,1536]{1,0:T(8,128)(2,1)} %bitcast.237, bf16[1536,1536]{1,0:T(8,128)(2,1)} %param.11), kind=kOutput, calls=%fused_computation.24 | convolution fusion | flops 2415919104 | bytes 9437184 | tf_op jit(solution)/shard_map/dot_general | solution.py:186
  234.0 3.6 copy.180
  237.6 2.8 reshape.200
  240.4 3.9 all-to-all-done
  252.0 3.3 fusion.96
  269.8 4.4 all-to-all-start.4
  274.2 4.2 bitcast_reduce_fusion
  284.1 6.0 all-to-all-start.5
  297.1 29.3 %all-to-all-done.5 = bf16[128,24,2,128]{3,1,2,0:T(8,128)(2,1)} async-done(((bf16[128,24,2,128]{3,1,2,0:T(8,128)(2,1)}), bf16[128,24,2,128]{3,1,2,0:T(8,128)(2,1)}, u32[]{:S(2)}, u32[]{:S(2)}) %all-to-all-start.5) | async-done | bytes 1572896 | tf_op jit(solution)/shard_map/all_to_all | solution.py:227
  326.5 3.0 copy.198
  329.5 3.1 reduce_sum.191
  338.1 12.2 %all-gather.12.cloned.1.call-done = bf16[1152,512]{1,0:T(8,128)(2,1)} async-done(((bf16[1152,128]{1,0:T(8,128)(2,1)}), bf16[1152,512]{1,0:T(8,128)(2,1)}) %all-gather.12.cloned.1.call-update) | async-done | bytes 1179664 | tf_op jit(solution)/shard_map/all_gather | solution.py:233
  350.3 5.2 fusion.109
  355.4 16.7 %all-gather.14.cloned.1.call-done = bf16[1536,512]{0,1:T(8,128)(2,1)} async-done(((bf16[1536,128]{0,1:T(8,128)(2,1)}), bf16[1536,512]{0,1:T(8,128)(2,1)}) %all-gather.14.cloned.1.call-update) | async-done | bytes 1572880 | tf_op jit(solution)/shard_map/all_gather | solution.py:234
  372.1 8.0 %convolution_add_fusion.1 = f32[512,1536]{1,0:T(8,128)} fusion(f32[512,1536]{1,0:T(8,128)} %fusion.109, bf16[1536,512]{0,1:T(8,128)(2,1)} %all-gather.14.cloned.1.call-done, bf16[1536,1536]{1,0:T(8,128)(2,1)} %param.11), kind=kOutput, calls=%fused_computation.26 | convolution fusion | flops 2416705536 | bytes 12582912 | tf_op jit(solution)/shard_map/dot_general | solution.py:239
  380.2 3.9 reshape.195
  394.5 5.5 all-to-all-start.2
  403.2 4.1 all-to-all-done.2
  409.8 6.3 %all_gather.34 = bf16[384,512]{1,0:T(8,128)(2,1)S(1)} all-gather(bf16[384,128]{1,0:T(8,128)(2,1)S(1)} %reshape.183), channel_id=1, replica_groups=mesh['dp'=4,'mp'=8] {'dp'}, dimensions={1}, use_global_device_ids=true | all-gather | bytes 491520 | tf_op jit(solution)/shard_map/all_gather | solution.py:203
  421.7 5.3 fusion.107
  427.1 2.7 convolution_add_fusion
  429.8 3.9 reshape.185
  437.4 4.0 fusion.13
  444.4 3.6 convolution_convert_fusion.4
  452.3 5.9 add_convert_fusion
  458.2 5.0 add_convert_fusion.1
  465.5 4.0 fusion.5
  469.4 2.8 reduce-scatter.17.cloned.1.call-done
  472.2 4.6 collective-permute-start.3
  476.8 6.3 %fusion.3 = bf16[1152,1536]{1,0:T(8,128)(2,1)} fusion(f32[1152,1536]{1,0:T(8,128)} %fusion.5, bf16[128,1536]{0,1:T(8,128)(2,1)} %bitcast.211, bf16[1152,512]{1,0:T(8,128)(2,1)} %all-gather.12.cloned.1.call-done), kind=kOutput, calls=%fused_computation.6 | convolution fusion | flops 460062720 | bytes 11304960 | tf_op jit(solution)/shard_map/dot_general | solution.py:149
  483.1 77.0 %reduce-scatter.11.cloned.1.call-done = f32[1,128,768]{2,1,0:T(8,128)} async-done(((f32[8,128,768]{2,1,0:T(8,128)}), f32[1,128,768]{2,1,0:T(8,128)}) %reduce-scatter.11.cloned.1.call-update) | async-done | bytes 393232 | tf_op jit(solution)/shard_map/reduce_scatter | solution.py:141
  560.1 4.5 collective-permute-start.1
  566.4 6.8 %psum.23 = f32[768]{0:T(1024)} all-reduce(f32[768]{0:T(1024)S(1)} %get-tuple-element.9), channel_id=1, replica_groups=mesh['dp'=4,'mp'=8] {'dp'}, use_global_device_ids=true, to_apply=%region_27.0 | all-reduce | flops 768 | bytes 6144 | tf_op jit(solution)/shard_map/psum | solution.py:251
  573.2 20.9 %all-reduce = (f32[128]{0:T(128)}, f32[128]{0:T(128)}) all-reduce(f32[128]{0:T(128)} %get-tuple-element.10, f32[128]{0:T(128)} %get-tuple-element.11), channel_id=1, replica_groups=mesh['dp'=4,'mp'=8] {'mp'}, use_global_device_ids=true, to_apply=%region_25.0 | all-reduce | flops 256 | bytes 2048 | tf_op jit(solution)/shard_map/psum | solution.py:243
  (207 shorter events, 137.0 us)
Async XLA Ops:
  7.2 110.9 %copy-start = (bf16[3,16,24,1536]{3,2,1,0:T(8,128)(2,1)S(1)}, bf16[3,16,24,1536]{3,2,1,0:T(8,128)(2,1)}, u32[]{:S(2)}) copy-start(bf16[3,16,24,1536]{3,2,1,0:T(8,128)(2,1)} %param.9) | copy-start | bytes 10616836
  7.2 61.2 %all-gather.18.cloned.1.call-start = ((), (), s32[]{:S(2)}) async-start(), calls=%async_computation.22 | async-start | bytes 1769472 | tf_op jit(solution)/shard_map/all_gather | solution.py:130
  7.2 3.4 collective-permute-start.2
  10.6 104.1 %all-gather.16.cloned.1.call-start = ((), (), s32[]{:S(2)}) async-start(), calls=%async_computation.21 | async-start | bytes 1769472 | tf_op jit(solution)/shard_map/all_gather | solution.py:130
  44.6 26.8 %copy-start.34 = (f32[128]{0:T(128)}, f32[128]{0:T(128)S(1)}, u32[]{:S(2)}) copy-start(f32[128]{0:T(128)S(1)} %broadcast_multiply_fusion.8) | copy-start | bytes 1540
  44.6 26.8 %copy-start.36 = (f32[128]{0:T(128)}, f32[128]{0:T(128)S(1)}, u32[]{:S(2)}) copy-start(f32[128]{0:T(128)S(1)} %add_rsqrt_fusion.2) | copy-start | bytes 1540
  45.7 1.3 collective-permute-start
  47.1 92.9 %reduce-scatter.13.cloned.1.call-start = ((), (), s32[]{:S(2)}) async-start(), calls=%async_computation.16 | async-start | bytes 983040 | tf_op jit(solution)/shard_map/reduce_scatter | solution.py:221
  71.4 1.4 copy-start.29
  74.6 101.7 %reduce-scatter.7.cloned.1.call-start = ((), (), s32[]{:S(2)}) async-start(), calls=%async_computation.12 | async-start | bytes 2949120 | tf_op jit(solution)/shard_map/reduce_scatter | solution.py:184
  122.9 211.6 %reduce-scatter.15.cloned.1.call-start = ((), (), s32[]{:S(2)}) async-start(), calls=%async_computation.18 | async-start | bytes 3932160 | tf_op jit(solution)/shard_map/reduce_scatter | solution.py:216
  149.0 38.8 %all-to-all-start.3 = ((bf16[8,2,3072]{2,1,0:T(2,128)(2,1)}), bf16[8,2,3072]{2,1,0:T(2,128)(2,1)}, u32[]{:S(2)}, u32[]{:S(2)}) async-start(bf16[8,2,3072]{2,1,0:T(2,128)(2,1)} %reshape.215), calls=%async_computation.7 | async-start | bytes 196608 | tf_op jit(solution)/shard_map/all_to_all | solution.py:223
  187.8 13.0 %all-to-all-start.1 = ((bf16[8,2,3072]{2,1,0:T(2,128)(2,1)}), bf16[8,2,3072]{2,1,0:T(2,128)(2,1)}, u32[]{:S(2)}, u32[]{:S(2)}) async-start(bf16[8,2,3072]{2,1,0:T(2,128)(2,1)} %reshape.211), calls=%async_computation.2 | async-start | bytes 196608 | tf_op jit(solution)/shard_map/all_to_all | solution.py:196
  203.7 40.6 %all-to-all-start = ((bf16[16,192,2,128]{3,2,0,1:T(2,128)(2,1)}), bf16[16,192,2,128]{3,2,0,1:T(2,128)(2,1)}, u32[]{:S(2)}, u32[]{:S(2)}) async-start(bf16[16,192,2,128]{3,2,0,1:T(2,128)(2,1)} %bitcast.205), calls=%async_computation.1 | async-start | bytes 3145728 | tf_op jit(solution)/shard_map/all_to_all | solution.py:197
  208.0 126.5 %reduce-scatter.9.cloned.1.call-start = ((), (), s32[]{:S(2)}) async-start(), calls=%async_computation.13 | async-start | bytes 3932160 | tf_op jit(solution)/shard_map/reduce_scatter | solution.py:189
  229.5 1.7 copy-start.2
  269.8 14.3 %all-to-all-start.4 = ((bf16[8,2,3072]{2,1,0:T(2,128)(2,1)}), bf16[8,2,3072]{2,1,0:T(2,128)(2,1)}, u32[]{:S(2)}, u32[]{:S(2)}) async-start(bf16[8,2,3072]{2,1,0:T(2,128)(2,1)} %reshape.217), calls=%async_computation.8 | async-start | bytes 196608 | tf_op jit(solution)/shard_map/all_to_all | solution.py:226
  279.1 2.2 copy-start.32
  279.1 2.2 copy-start.33
  284.1 42.3 %all-to-all-start.5 = ((bf16[128,24,2,128]{3,1,2,0:T(8,128)(2,1)}), bf16[128,24,2,128]{3,1,2,0:T(8,128)(2,1)}, u32[]{:S(2)}, u32[]{:S(2)}) async-start(bf16[128,24,2,128]{3,1,2,0:T(8,128)(2,1)} %copy.197), calls=%async_computation.9 | async-start | bytes 3145728 | tf_op jit(solution)/shard_map/all_to_all | solution.py:227
  290.1 60.2 %all-gather.12.cloned.1.call-start = ((), (), s32[]{:S(2)}) async-start(), calls=%async_computation.17 | async-start | bytes 1474560 | tf_op jit(solution)/shard_map/all_gather | solution.py:233
  334.4 37.7 %all-gather.14.cloned.1.call-start = ((), (), s32[]{:S(2)}) async-start(), calls=%async_computation.19 | async-start | bytes 1966080 | tf_op jit(solution)/shard_map/all_gather | solution.py:234
  337.2 84.6 %all-gather.10.cloned.1.call-start = ((), (), s32[]{:S(2)}) async-start(), calls=%async_computation.14 | async-start | bytes 1966080 | tf_op jit(solution)/shard_map/all_gather | solution.py:204
  337.9 134.3 %reduce-scatter.17.cloned.1.call-start = ((), (), s32[]{:S(2)}) async-start(), calls=%async_computation.20 | async-start | bytes 3538944 | tf_op jit(solution)/shard_map/reduce_scatter | solution.py:141
  387.5 3.8 copy-start.4
  390.4 9.7 %copy-start.7 = (bf16[1024,768]{1,0:T(8,128)(2,1)S(1)}, bf16[1024,768]{1,0:T(8,128)(2,1)}, u32[]{:S(2)}) copy-start(bf16[1024,768]{1,0:T(8,128)(2,1)} %all-gather.16.cloned.1.call-done) | copy-start | bytes 4718596
  394.5 12.8 %all-to-all-start.2 = ((bf16[8,2,3072]{2,1,0:T(2,128)(2,1)}), bf16[8,2,3072]{2,1,0:T(2,128)(2,1)}, u32[]{:S(2)}, u32[]{:S(2)}) async-start(bf16[8,2,3072]{2,1,0:T(2,128)(2,1)} %reshape.213), calls=%async_computation.3 | async-start | bytes 196608 | tf_op jit(solution)/shard_map/all_to_all | solution.py:200
  400.1 160.0 %reduce-scatter.11.cloned.1.call-start = ((), (), s32[]{:S(2)}) async-start(), calls=%async_computation.15 | async-start | bytes 3538944 | tf_op jit(solution)/shard_map/reduce_scatter | solution.py:141
  400.4 47.5 %copy-start.10 = (bf16[1,128,2,768]{1,3,2,0:T(8,128)(2,1)}, bf16[1,128,2,768]{1,3,2,0:T(8,128)(2,1)S(1)}, u32[]{:S(2)}) copy-start(bf16[1,128,2,768]{1,3,2,0:T(8,128)(2,1)S(1)} %copy.206) | copy-start | bytes 1179652
  403.2 12.9 %copy-start.11 = (bf16[1,128,2,768]{1,3,2,0:T(8,128)(2,1)S(1)}, bf16[1,128,2,768]{1,3,2,0:T(8,128)(2,1)}, u32[]{:S(2)}) copy-start(bf16[1,128,2,768]{1,3,2,0:T(8,128)(2,1)} %copy.210) | copy-start | bytes 1179652
  409.8 8.2 %copy-start.13 = (bf16[1,128,2,768]{1,3,2,0:T(8,128)(2,1)S(1)}, bf16[1,128,2,768]{1,3,2,0:T(8,128)(2,1)}, u32[]{:S(2)}) copy-start(bf16[1,128,2,768]{1,3,2,0:T(8,128)(2,1)} %copy.209) | copy-start | bytes 1179652
  416.1 11.0 %copy-start.17 = (bf16[384,512]{1,0:T(8,128)(2,1)}, bf16[384,512]{1,0:T(8,128)(2,1)S(1)}, u32[]{:S(2)}) copy-start(bf16[384,512]{1,0:T(8,128)(2,1)S(1)} %all_gather.34) | copy-start | bytes 1179652
  418.0 1.9 copy-start.15
  421.7 5.3 copy-start.30
  435.7 1.7 copy-start.5
  435.7 1.7 copy-start.18
  437.4 4.1 copy-start.9
  437.4 4.1 copy-start.16
  444.4 3.6 copy-start.8
  449.4 1.4 copy-start.22
  450.9 1.4 copy-start.19
  458.2 5.0 copy-start.24
  458.2 5.0 copy-start.27
  472.2 92.3 %copy-start.35 = (f32[128]{0:T(128)S(1)}, f32[128]{0:T(128)}, u32[]{:S(2)}) copy-start(f32[128]{0:T(128)} %copy-done.34) | copy-start | bytes 1540
  472.2 92.3 %copy-start.37 = (f32[128]{0:T(128)S(1)}, f32[128]{0:T(128)}, u32[]{:S(2)}) copy-start(f32[128]{0:T(128)} %copy-done.36) | copy-start | bytes 1540
  472.2 92.3 %collective-permute-start.3 = (f32[128,768]{1,0:T(8,128)}, f32[128,768]{1,0:T(8,128)}, u32[]{:S(2)}, u32[]{:S(2)}) collective-permute-start(f32[128,768]{1,0:T(8,128)} %bitcast.249), channel_id=1, source_target_pairs={{0,0},{1,1},{2,8},{3,9},{4,16},{5,17},{6,24},{7,25},{8,2},{9,3},{1... | collective-permute-start | bytes 1179656 | tf_op jit(solution)/shard_map/ppermute | solution.py:123
  476.8 120.9 %copy-start.1 = (bf16[3,16,24,1536]{3,2,1,0:T(8,128)(2,1)S(1)}, bf16[3,16,24,1536]{3,2,1,0:T(8,128)(2,1)}, u32[]{:S(2)}) copy-start(bf16[3,16,24,1536]{3,2,1,0:T(8,128)(2,1)} %param.9) | copy-start | bytes 10616836
  560.1 35.3 %collective-permute-start.1 = (f32[128,768]{1,0:T(8,128)}, f32[128,768]{1,0:T(8,128)}, u32[]{:S(2)}, u32[]{:S(2)}) collective-permute-start(f32[128,768]{1,0:T(8,128)} %bitcast.250), channel_id=1, source_target_pairs={{0,0},{1,1},{2,8},{3,9},{4,16},{5,17},{6,24},{7,25},{8,2},{9,3},{1... | collective-permute-start | bytes 1179656 | tf_op jit(solution)/shard_map/ppermute | solution.py:123
  (11 other events, 13.2 us)
Sparse Core Ops, SparseCore 0:
  10.7 57.5 all-gather.17
  70.5 44.1 all-gather.15
  117.9 22.0 reduce-scatter.12
  143.1 33.0 reduce-scatter.6
  179.2 37.9 reduce-scatter.14
  220.3 37.9 reduce-scatter.8
  334.6 15.6 all-gather.11
  352.4 19.6 all-gather.13
  374.3 19.6 all-gather.9
  398.0 74.2 reduce-scatter.16
  475.8 84.2 reduce-scatter.10

commit v2 on v1

--- a/solution.py
+++ b/solution.py
@@ -178,30 +178,49 @@
     hidden_all = spread_quarter(hidden_local)
     cot_all = spread_quarter(cotangent)
 
-    projected = lax.dot_general(
-        qkv_flat, hidden_all, contract_cols, preferred_element_type=jnp.float32
-    )
-    projected = lax.psum_scatter(projected, "dp", scatter_dimension=1, tiled=True)
-    projected = projected.astype(jnp.bfloat16).reshape(3, head_slice, HEADS, ROWS)
-    up_input = lax.dot_general(
-        up_weight, hidden_all, contract_cols, preferred_element_type=jnp.float32
-    )
-    up_input = lax.psum_scatter(up_input, "dp", scatter_dimension=1, tiled=True)
+    n_proj = qkv_flat.shape[0]
+    proj_up = jnp.concatenate(
+        [
+            lax.dot_general(qkv_flat, hidden_all, contract_cols, preferred_element_type=jnp.float32),
+            lax.dot_general(up_weight, hidden_all, contract_cols, preferred_element_type=jnp.float32),
+        ],
+        axis=0,
+    )
+    proj_up = lax.psum_scatter(proj_up, "dp", scatter_dimension=1, tiled=True)
+    projected = proj_up[:n_proj].astype(jnp.bfloat16).reshape(3, head_slice, HEADS, ROWS)
+    up_input = proj_up[n_proj:]
     activated, gelu_slope = gelu_pair(up_input)
     up_output = activated.astype(jnp.bfloat16)
 
-    queries = projected[0].reshape(head_slice, ITEMS, TQ)
-    keyvals = to_items(projected[1:])
-    query_heads, pair_heads = (
-        lax.all_to_all(queries, "mp", split_axis=1, concat_axis=0, tiled=True),
-        lax.all_to_all(keyvals, "mp", split_axis=1, concat_axis=0, tiled=True),
-    )
-    attended, stored = attend(query_heads, pair_heads)
-    head_rows = lax.all_to_all(attended, "mp", split_axis=0, concat_axis=1, tiled=True).reshape(
-        head_slice * HEADS, ROWS
-    )
-    head_rows_all = lax.all_gather(head_rows, "dp", axis=1, tiled=True)
-    up_output_all = lax.all_gather(up_output, "dp", axis=1, tiled=True)
+    by_head = HEADS % n_mp == 0
+    if by_head:
+        head_group = HEADS // n_mp
+        qkv_heads = lax.all_to_all(projected, "mp", split_axis=2, concat_axis=1, tiled=True)
+        query_heads = qkv_heads[0].reshape(HS, head_group * QB, TQ)
+        pairs = jnp.stack([qkv_heads[1], qkv_heads[2]], axis=2)
+        pair_heads = jnp.broadcast_to(
+            pairs[:, :, None], (HS, head_group, QB, 2, PATCHES)
+        ).reshape(HS, head_group * QB, 2, PATCHES)
+        attended, stored = attend(query_heads, pair_heads)
+        head_rows = lax.all_to_all(
+            attended.reshape(HS, head_group, ROWS), "mp", split_axis=0, concat_axis=1, tiled=True
+        ).reshape(head_slice * HEADS, ROWS)
+    else:
+        queries = projected[0].reshape(head_slice, ITEMS, TQ)
+        keyvals = to_items(projected[1:])
+        query_heads, pair_heads = (
+            lax.all_to_all(queries, "mp", split_axis=1, concat_axis=0, tiled=True),
+            lax.all_to_all(keyvals, "mp", split_axis=1, concat_axis=0, tiled=True),
+        )
+        attended, stored = attend(query_heads, pair_heads)
+        head_rows = lax.all_to_all(attended, "mp", split_axis=0, concat_axis=1, tiled=True).reshape(
+            head_slice * HEADS, ROWS
+        )
+    n_att = head_rows.shape[0]
+    both_all = lax.all_gather(
+        jnp.concatenate([head_rows, up_output], axis=0), "dp", axis=1, tiled=True
+    )
+    head_rows_all, up_output_all = both_all[:n_att], both_all[n_att:]
     branch = lax.dot_general(
         head_rows_all, head_flat, contract_rows, preferred_element_type=jnp.float32
     ) + lax.dot_general(up_output_all, down_weight, contract_rows, preferred_element_type=jnp.float32)
@@ -210,28 +229,45 @@
 
     down_grad = blockwise_grad(up_output_all, cot_all, n_dp)
     head_grad = blockwise_grad(head_rows_all, cot_all, n_dp)
-    up_back = lax.dot_general(
-        down_weight, cot_all, contract_cols, preferred_element_type=jnp.float32
-    )
-    up_back = lax.psum_scatter(up_back, "dp", scatter_dimension=1, tiled=True)
-    up_upstream = (up_back * gelu_slope).astype(jnp.bfloat16)
-    head_upstream = lax.dot_general(
-        head_flat, cot_all, contract_cols, preferred_element_type=jnp.float32
-    )
-    head_upstream = lax.psum_scatter(head_upstream, "dp", scatter_dimension=1, tiled=True)
-    head_upstream = head_upstream.astype(jnp.bfloat16).reshape(head_slice, ITEMS, TQ)
-    upstream = lax.all_to_all(head_upstream, "mp", split_axis=1, concat_axis=0, tiled=True)
-    query_grad, pair_grad = attend_back(upstream, stored)
-    query_local, pair_local = (
-        lax.all_to_all(query_grad, "mp", split_axis=0, concat_axis=1, tiled=True),
-        lax.all_to_all(pair_grad, "mp", split_axis=0, concat_axis=1, tiled=True),
-    )
-    proj_grad = jnp.concatenate(
-        [query_local.reshape(1, head_slice, HEADS, ROWS), from_items(pair_local)], axis=0
-    )
+    back = jnp.concatenate(
+        [
+            lax.dot_general(head_flat, cot_all, contract_cols, preferred_element_type=jnp.float32),
+            lax.dot_general(down_weight, cot_all, contract_cols, preferred_element_type=jnp.float32),
+        ],
+        axis=0,
+    )
+    back = lax.psum_scatter(back, "dp", scatter_dimension=1, tiled=True)
+    up_upstream = (back[n_att:] * gelu_slope).astype(jnp.bfloat16)
+    head_upstream = back[:n_att].astype(jnp.bfloat16).reshape(head_slice, HEADS, ROWS)
+    if by_head:
+        upstream = lax.all_to_all(
+            head_upstream, "mp", split_axis=1, concat_axis=0, tiled=True
+        ).reshape(HS, head_group * QB, TQ)
+        query_grad, pair_grad = attend_back(upstream, stored)
+        pair_sum = jnp.sum(
+            pair_grad.reshape(HS, head_group, QB, 2, PATCHES).astype(jnp.float32), axis=2
+        ).astype(jnp.bfloat16)
+        grads = jnp.stack(
+            [query_grad.reshape(HS, head_group, ROWS), pair_sum[:, :, 0], pair_sum[:, :, 1]]
+        )
+        proj_grad = lax.all_to_all(grads, "mp", split_axis=1, concat_axis=2, tiled=True)
+    else:
+        upstream = lax.all_to_all(
+            head_upstream.reshape(head_slice, ITEMS, TQ), "mp", split_axis=1, concat_axis=0, tiled=True
+        )
+        query_grad, pair_grad = attend_back(upstream, stored)
+        query_local, pair_local = (
+            lax.all_to_all(query_grad, "mp", split_axis=0, concat_axis=1, tiled=True),
+            lax.all_to_all(pair_grad, "mp", split_axis=0, concat_axis=1, tiled=True),
+        )
+        proj_grad = jnp.concatenate(
+            [query_local.reshape(1, head_slice, HEADS, ROWS), from_items(pair_local)], axis=0
+        )
     proj_grad = proj_grad.reshape(3 * head_slice * HEADS, ROWS)
-    proj_grad_all = lax.all_gather(proj_grad, "dp", axis=1, tiled=True)
-    up_upstream_all = lax.all_gather(up_upstream, "dp", axis=1, tiled=True)
+    grads_all = lax.all_gather(
+        jnp.concatenate([proj_grad, up_upstream], axis=0), "dp", axis=1, tiled=True
+    )
+    proj_grad_all, up_upstream_all = grads_all[:n_proj], grads_all[n_proj:]
     qkv_grad = blockwise_grad(proj_grad_all, hidden_all, n_dp)
     up_grad = blockwise_grad(up_upstream_all, hidden_all, n_dp)
     input_partial = lax.dot_general(

time: 616 us -> 564 us (0.916)
  local copies, waits for them, and re-layouts: 110 us -> 71.5 us
  matrix products: 97.6 us -> 75.4 us
  waiting for transfers between devices: 242 us -> 262 us
  starting transfers between devices: 45.8 us -> 29.6 us
    reduce_scatter x4 -> x2, waiting for transfers between devices: 31.4 us -> 78.8 us  [the longest x1 45.4 us: shards(): proj_up = lax.psum_scatter(proj_up, 'dp', scatter_dimension=1, tiled=True)]
    reduce_scatter x2, waiting for transfers between devices: 79.7 us -> 108 us  [gather_quarter(): summed = lax.psum_scatter(pieces, 'mp', scatter_dimension=0, tiled=True)]
    all_to_all x5 -> x2, waiting for transfers between devices: 39.3 us -> 13.4 us  [the longest x1 8.21 us: shards(): lax.all_to_all(grads, 'mp', split_axis=1, concat_axis=2, tiled=True)]
    all_gather x3 -> x2, waiting for transfers between devices: 28.8 us -> 3.48 us  [the longest x1 3.48 us: shards(): lax.all_gather(jnp.concatenate([proj_grad, up_upstream], axis=0), 'dp', a...]
    unnamed x86 -> x64, local copies, waits for them, and re-layouts: 24.5 us -> 4.58 us
    all_to_all x5 -> x2, starting transfers between devices: 25.9 us -> 9.82 us  [the longest x1 5.72 us: shards(): lax.all_to_all(projected, 'mp', split_axis=2, concat_axis=1, tiled=True)]
    all_to_all x0 -> x1, blocking collectives: none -> 11 us  [shards(): lax.all_to_all(attended.reshape(HS, head_group, ROWS), 'mp', split_axis=0...]
    dot_general x16, matrix products: 43.7 us -> 32.9 us  [blockwise_grad(): jnp.dot(left[:, block * rows:(block + 1) * rows], right[block * rows:(blo...]
  transfers between devices with their start and end apart: 21 -> 15, of which waited for: 12 -> 9; matrix products, arithmetic and copies ran while one was open for 37% -> 23% of each run, Pallas kernels for 0% -> 0%
where the time goes in v2:
time: 564 us; the launch traced here: 554 us
  waiting for transfers between devices  262 us (46%)
  matrix products  75.4 us (13%)
  local copies, waits for them, and re-layouts  71.5 us (13%)
  blocking collectives  69.5 us (12%)
  other arithmetic  30.2 us (5%)
  starting transfers between devices  29.6 us (5%)
  between operations  15.2 us (3%)
    reduce_scatter x2, waiting for transfers between devices, gather_quarter(): summed = lax.psum_scatter(pieces, 'mp', scatter_dimension=0, tiled=True)  108 us
    all_gather x2, waiting for transfers between devices, spread_quarter(): pieces = lax.all_gather(swap(block), 'mp', axis=0, tiled=False)  58.2 us
    reduce_scatter x1, waiting for transfers between devices, shards(): proj_up = lax.psum_scatter(proj_up, 'dp', scatter_dimension=1, tiled=True)  45.4 us
    reduce_scatter x1, waiting for transfers between devices, shards(): back = lax.psum_scatter(back, 'dp', scatter_dimension=1, tiled=True)  33.3 us
    dot_general x16, matrix products, blockwise_grad(): jnp.dot(left[:, block * rows:(block + 1) * rows], right[block * rows:(blo...  32.9 us
    all_gather x1, blocking collectives, shards(): lax.all_gather(jnp.stack([block_mean, block_m2]), 'mp', axis=0, tiled=False)  31 us
    psum x1, blocking collectives, shards(): lax.psum((jnp.sum(scaled, axis=1), jnp.sum(scaled * normed, axis=1)), 'mp')  20.6 us
    ppermute x4, starting transfers between devices, swap(): return lax.ppermute(block, ('dp', 'mp'), swap_pairs(n_dp, n_mp))  13.8 us
  transfers between devices with their start and end apart: 15, of which 9 were waited for; matrix products, arithmetic and copies ran while one was open for 23% of the time, Pallas kernels for 0%

profile of v2, /device:TPU:0, one launch (start us, length us, event | category | flops | bytes accessed | tf_op | source)
XLA Modules:
  0.0 553.6 jit_solution(13545724215293245136)
XLA Ops:
  7.2 3.4 collective-permute-start.2
  13.5 31.0 %all-gather.3 = f32[8,2,128]{2,1,0:T(2,128)S(1)} all-gather(f32[1,2,128]{2,1,0:T(2,128)S(1)} %maximum_bitcast_fusion), channel_id=2, replica_groups=mesh['dp'=4,'mp'=8] {'mp'}, dimensions={0}, use_global_device_ids=true | all-gather | bytes 9216 | tf_op jit(solution)/shard_map/all_gather | solution.py:170
  47.2 21.2 %all-gather.15.cloned.1.call-done = bf16[1024,768]{1,0:T(8,128)(2,1)} async-done(((bf16[128,768]{1,0:T(8,128)(2,1)}), bf16[1024,768]{1,0:T(8,128)(2,1)}) %all-gather.15.cloned.1.call-update) | async-done | bytes 1572880 | tf_op jit(solution)/shard_map/all_gather | solution.py:130
  68.4 3.2 copy.114
  72.8 2.6 fusion.110
  75.5 2.2 pad_maximum_fusion.1
  77.7 37.0 %all-gather.13.cloned.1.call-done = bf16[1024,768]{1,0:T(8,128)(2,1)} async-done(((bf16[128,768]{1,0:T(8,128)(2,1)}), bf16[1024,768]{1,0:T(8,128)(2,1)}) %all-gather.13.cloned.1.call-update) | async-done | bytes 1572880 | tf_op jit(solution)/shard_map/all_gather | solution.py:130
  114.8 3.0 copy.102
  118.1 2.2 convolution_bitcast_fusion.1
  120.4 2.6 convolution_bitcast_fusion
  123.0 3.3 pad_maximum_fusion
  126.3 33.3 %reduce-scatter.9.cloned.1.call-done = f32[1920,128]{0,1:T(8,128)} async-done(((f32[1920,512]{0,1:T(8,128)}), f32[1920,128]{0,1:T(8,128)}) %reduce-scatter.9.cloned.1.call-update) | async-done | bytes 983056 | tf_op jit(solution)/shard_map/reduce_scatter | solution.py:239
  164.4 5.5 all-to-all-start.2
  169.9 45.4 %reduce-scatter.5.cloned.1.call-done = f32[2688,128]{0,1:T(8,128)} async-done(((f32[2688,512]{0,1:T(8,128)}), f32[2688,128]{0,1:T(8,128)}) %reduce-scatter.5.cloned.1.call-update) | async-done | bytes 1376272 | tf_op jit(solution)/shard_map/reduce_scatter | solution.py:189
  220.7 5.7 %all-to-all-start = ((bf16[3,16,24,128]{3,1,0,2:T(8,128)(2,1)}), bf16[3,16,24,128]{3,1,0,2:T(8,128)(2,1)}, u32[]{:S(2)}, u32[]{:S(2)}) async-start(bf16[3,16,24,128]{3,1,0,2:T(8,128)(2,1)} %copy.104), calls=%async_computation.1 | async-start | bytes 589824 | tf_op jit(solution)/shard_map/all_to_all | solution.py:198
  226.4 2.1 copy.119
  228.6 2.3 reshape.208
  230.9 5.2 all-to-all-done
  245.3 2.5 copy.108
  247.9 2.5 reshape.215
  253.5 2.4 convolution_convert_fusion.16
  256.0 3.3 fusion.102
  259.2 4.1 bitcast_reduce_fusion
  268.5 2.1 fusion.26
  271.9 4.1 all-to-all-start.3
  276.1 2.6 fusion.44
  278.7 8.2 %all-to-all-done.3 = bf16[3,128,3,128]{3,2,0,1:T(4,128)(2,1)} async-done(((bf16[3,128,3,128]{3,2,0,1:T(4,128)(2,1)}), bf16[3,128,3,128]{3,2,0,1:T(4,128)(2,1)}, u32[]{:S(2)}, u32[]{:S(2)}) %all-to-all-start.3) | async-done | bytes 294944 | tf_op jit(solution)/shard_map/all_to_all | solution.py:253
  294.8 2.5 convolution_convert_fusion.17
  298.9 11.0 %all_to_all.60 = bf16[128,3,128]{2,1,0:T(4,128)(2,1)S(1)} all-to-all(bf16[128,3,128]{2,1,0:T(4,128)(2,1)} %copy.109), channel_id=1, replica_groups=mesh['dp'=4,'mp'=8] {'mp'}, dimensions={0} | all-to-all | bytes 196608 | tf_op jit(solution)/shard_map/all_to_all | solution.py:205
  315.9 3.5 all-gather.11.cloned.1.call-done
  319.4 3.6 fusion.31
  323.0 6.7 %convolution_add_fusion.1 = f32[512,1536]{1,0:T(8,128)} fusion(f32[512,1536]{1,0:T(8,128)S(1)} %fusion.31, bf16[1536,1536]{1,0:T(8,128)(2,1)} %param.11, bf16[2688,512]{0,1:T(8,128)(2,1)S(1)} %copy-done.6), kind=kOutput, calls=%fused_computation.28 | convolution fusion | flops 2416705536 | bytes 12582912 | tf_op jit(solution)/shard_map/dot_general | solution.py:275
  329.7 3.8 reshape.210
  347.7 5.0 fusion.29
  352.8 3.6 convolution_add_fusion
  356.4 3.8 reshape.202
  360.3 2.0 copy.113
  372.0 4.1 add_convert_fusion
  382.7 4.0 fusion.5
  386.7 3.9 add_convert_fusion.1
  390.6 31.3 %reduce-scatter.11.cloned.1.call-done = f32[1,128,768]{2,1,0:T(8,128)} async-done(((f32[8,128,768]{2,1,0:T(8,128)}), f32[1,128,768]{2,1,0:T(8,128)}) %reduce-scatter.11.cloned.1.call-update) | async-done | bytes 393232 | tf_op jit(solution)/shard_map/reduce_scatter | solution.py:141
  421.9 4.6 collective-permute-start.3
  426.5 6.3 %fusion.3 = bf16[1152,1536]{1,0:T(8,128)(2,1)} fusion(f32[1152,1536]{1,0:T(8,128)} %fusion.5, bf16[128,1536]{0,1:T(8,128)(2,1)} %bitcast.171, bf16[2688,512]{0,1:T(8,128)(2,1)} %all-gather.11.cloned.1.call-done), kind=kOutput, calls=%fused_computation.6 | convolution fusion | flops 460062720 | bytes 11304960 | tf_op jit(solution)/shard_map/dot_general | solution.py:149
  432.8 76.9 %reduce-scatter.7.cloned.1.call-done = f32[1,128,768]{2,1,0:T(8,128)} async-done(((f32[8,128,768]{2,1,0:T(8,128)}), f32[1,128,768]{2,1,0:T(8,128)}) %reduce-scatter.7.cloned.1.call-update) | async-done | bytes 393232 | tf_op jit(solution)/shard_map/reduce_scatter | solution.py:141
  509.7 4.5 collective-permute-start.1
  515.9 6.8 %psum.23 = f32[768]{0:T(1024)} all-reduce(f32[768]{0:T(1024)S(1)} %get-tuple-element.9), channel_id=1, replica_groups=mesh['dp'=4,'mp'=8] {'dp'}, use_global_device_ids=true, to_apply=%region_25.0 | all-reduce | flops 768 | bytes 6144 | tf_op jit(solution)/shard_map/psum | solution.py:287
  522.8 20.6 %all-reduce = (f32[128]{0:T(128)}, f32[128]{0:T(128)S(1)}) all-reduce(f32[128]{0:T(128)} %get-tuple-element.10, f32[128]{0:T(128)} %get-tuple-element.11), channel_id=1, replica_groups=mesh['dp'=4,'mp'=8] {'mp'}, use_global_device_ids=true, to_apply=%region_23.0 | all-reduce | flops 256 | bytes 2048 | tf_op jit(solution)/shard_map/psum | solution.py:279
  544.1 2.3 fusion.59
  (170 shorter events, 84.2 us)
Async XLA Ops:
  7.2 110.9 %copy-start = (bf16[3,16,24,1536]{3,2,1,0:T(8,128)(2,1)S(1)}, bf16[3,16,24,1536]{3,2,1,0:T(8,128)(2,1)}, u32[]{:S(2)}) copy-start(bf16[3,16,24,1536]{3,2,1,0:T(8,128)(2,1)} %param.9) | copy-start | bytes 10616836
  7.2 61.2 %all-gather.15.cloned.1.call-start = ((), (), s32[]{:S(2)}) async-start(), calls=%async_computation.15 | async-start | bytes 1769472 | tf_op jit(solution)/shard_map/all_gather | solution.py:130
  7.2 3.4 collective-permute-start.2
  10.6 104.1 %all-gather.13.cloned.1.call-start = ((), (), s32[]{:S(2)}) async-start(), calls=%async_computation.14 | async-start | bytes 1769472 | tf_op jit(solution)/shard_map/all_gather | solution.py:130
  44.6 2.5 copy-start.23
  44.6 2.5 copy-start.25
  45.7 1.4 collective-permute-start
  47.1 112.5 %reduce-scatter.9.cloned.1.call-start = ((), (), s32[]{:S(2)}) async-start(), calls=%async_computation.11 | async-start | bytes 4915200 | tf_op jit(solution)/shard_map/reduce_scatter | solution.py:239
  68.4 3.5 copy-start.18
  68.4 4.5 slice-start.2
  71.5 1.3 slice-start.3
  77.7 137.6 %reduce-scatter.5.cloned.1.call-start = ((), (), s32[]{:S(2)}) async-start(), calls=%async_computation.8 | async-start | bytes 6881280 | tf_op jit(solution)/shard_map/reduce_scatter | solution.py:189
  117.8 2.5 slice-start
  118.1 2.3 slice-start.1
  164.4 56.3 %all-to-all-start.2 = ((bf16[16,24,128]{2,0,1:T(8,128)(2,1)}), bf16[16,24,128]{2,0,1:T(8,128)(2,1)}, u32[]{:S(2)}, u32[]{:S(2)}) async-start(bf16[16,24,128]{2,0,1:T(8,128)(2,1)} %copy.118), calls=%async_computation.5 | async-start | bytes 196608 | tf_op jit(solution)/shard_map/all_to_all | solution.py:243
  220.7 15.4 %all-to-all-start = ((bf16[3,16,24,128]{3,1,0,2:T(8,128)(2,1)}), bf16[3,16,24,128]{3,1,0,2:T(8,128)(2,1)}, u32[]{:S(2)}, u32[]{:S(2)}) async-start(bf16[3,16,24,128]{3,1,0,2:T(8,128)(2,1)} %copy.104), calls=%async_computation.1 | async-start | bytes 589824 | tf_op jit(solution)/shard_map/all_to_all | solution.py:198
  237.1 0.7 copy-start.17
  240.9 3.4 copy-start.20
  243.2 1.1 copy-start.2
  252.0 0.7 copy-start.22
  267.7 2.9 copy-start.16
  267.7 3.2 copy-start.21
  271.9 15.0 %all-to-all-start.3 = ((bf16[3,128,3,128]{3,2,0,1:T(4,128)(2,1)}), bf16[3,128,3,128]{3,2,0,1:T(4,128)(2,1)}, u32[]{:S(2)}, u32[]{:S(2)}) async-start(bf16[3,128,3,128]{3,2,0,1:T(4,128)(2,1)} %copy.121), calls=%async_computation.6 | async-start | bytes 786432 | tf_op jit(solution)/shard_map/all_to_all | solution.py:253
  276.0 43.3 %all-gather.11.cloned.1.call-start = ((), (), s32[]{:S(2)}) async-start(), calls=%async_computation.12 | async-start | bytes 3440640 | tf_op jit(solution)/shard_map/all_gather | solution.py:267
  294.7 53.0 %all-gather.9.cloned.1.call-start = ((), (), s32[]{:S(2)}) async-start(), calls=%async_computation.9 | async-start | bytes 2457600 | tf_op jit(solution)/shard_map/all_gather | solution.py:220
  315.8 106.0 %reduce-scatter.11.cloned.1.call-start = ((), (), s32[]{:S(2)}) async-start(), calls=%async_computation.13 | async-start | bytes 3538944 | tf_op jit(solution)/shard_map/reduce_scatter | solution.py:141
  319.4 3.6 copy-start.6
  335.5 1.4 copy-start.3
  335.5 9.1 %copy-start.4 = (bf16[1024,768]{1,0:T(8,128)(2,1)S(1)}, bf16[1024,768]{1,0:T(8,128)(2,1)}, u32[]{:S(2)}) copy-start(bf16[1024,768]{1,0:T(8,128)(2,1)} %all-gather.13.cloned.1.call-done) | copy-start | bytes 4718596
  335.5 174.1 %reduce-scatter.7.cloned.1.call-start = ((), (), s32[]{:S(2)}) async-start(), calls=%async_computation.10 | async-start | bytes 3538944 | tf_op jit(solution)/shard_map/reduce_scatter | solution.py:141
  345.0 31.1 %copy-start.8 = (bf16[1,128,2,768]{1,3,2,0:T(8,128)(2,1)}, bf16[1,128,2,768]{1,3,2,0:T(8,128)(2,1)S(1)}, u32[]{:S(2)}) copy-start(bf16[1,128,2,768]{1,3,2,0:T(8,128)(2,1)S(1)} %copy.129) | copy-start | bytes 1179652
  347.7 5.0 copy-start.19
  362.3 1.0 copy-start.11
  362.3 2.4 copy-start.5
  364.7 1.4 copy-start.9
  366.1 1.0 copy-start.10
  369.0 1.4 copy-start.12
  372.0 4.1 copy-start.7
  376.1 1.4 copy-start.13
  377.6 1.4 copy-start.15
  379.0 1.4 copy-start.14
  421.9 92.2 %copy-start.24 = (f32[128]{0:T(128)S(1)}, f32[128]{0:T(128)}, u32[]{:S(2)}) copy-start(f32[128]{0:T(128)} %copy-done.23) | copy-start | bytes 1540
  421.9 92.2 %copy-start.26 = (f32[128]{0:T(128)S(1)}, f32[128]{0:T(128)}, u32[]{:S(2)}) copy-start(f32[128]{0:T(128)} %copy-done.25) | copy-start | bytes 1540
  421.9 92.2 %collective-permute-start.3 = (f32[128,768]{1,0:T(8,128)}, f32[128,768]{1,0:T(8,128)}, u32[]{:S(2)}, u32[]{:S(2)}) collective-permute-start(f32[128,768]{1,0:T(8,128)} %bitcast.213), channel_id=1, source_target_pairs={{0,0},{1,1},{2,8},{3,9},{4,16},{5,17},{6,24},{7,25},{8,2},{9,3},{1... | collective-permute-start | bytes 1179656 | tf_op jit(solution)/shard_map/ppermute | solution.py:123
  426.5 119.9 %copy-start.1 = (bf16[3,16,24,1536]{3,2,1,0:T(8,128)(2,1)S(1)}, bf16[3,16,24,1536]{3,2,1,0:T(8,128)(2,1)}, u32[]{:S(2)}) copy-start(bf16[3,16,24,1536]{3,2,1,0:T(8,128)(2,1)} %param.9) | copy-start | bytes 10616836
  509.7 34.4 %collective-permute-start.1 = (f32[128,768]{1,0:T(8,128)}, f32[128,768]{1,0:T(8,128)}, u32[]{:S(2)}, u32[]{:S(2)}) collective-permute-start(f32[128,768]{1,0:T(8,128)} %bitcast.214), channel_id=1, source_target_pairs={{0,0},{1,1},{2,8},{3,9},{4,16},{5,17},{6,24},{7,25},{8,2},{9,3},{1... | collective-permute-start | bytes 1179656 | tf_op jit(solution)/shard_map/ppermute | solution.py:123
Sparse Core Ops, SparseCore 0:
  10.7 57.5 all-gather.14
  70.5 44.1 all-gather.12
  117.9 41.7 reduce-scatter.8
  162.2 53.0 reduce-scatter.4
  294.9 24.4 all-gather.10
  321.4 21.8 all-gather.8
  347.4 74.4 reduce-scatter.10
  425.5 84.1 reduce-scatter.6

commit v3 on v2

--- a/solution.py
+++ b/solution.py
@@ -142,6 +142,16 @@
     return swap(summed.reshape(rows, width))
 
 
+def gather_quarter_exchange(partial, rows):
+    n_dp, n_mp = lax.axis_size("dp"), lax.axis_size("mp")
+    ratio = n_mp // n_dp
+    width = partial.shape[1] // ratio
+    pieces = partial.reshape(n_dp, rows, ratio, width)
+    pieces = jnp.transpose(pieces, (0, 2, 1, 3)).reshape(n_mp, rows, width)
+    received = lax.all_to_all(pieces, "mp", split_axis=0, concat_axis=0, tiled=True)
+    return swap(jnp.sum(received, axis=0))
+
+
 def blockwise_grad(left, right, n_blocks):
     rows = left.shape[1] // n_blocks
     total = None
@@ -176,7 +186,6 @@
     gain_wide = norm_gain.astype(jnp.float32)
     hidden_local = (normed * gain_wide).astype(jnp.bfloat16)
     hidden_all = spread_quarter(hidden_local)
-    cot_all = spread_quarter(cotangent)
 
     n_proj = qkv_flat.shape[0]
     proj_up = jnp.concatenate(
@@ -187,6 +196,8 @@
         axis=0,
     )
     proj_up = lax.psum_scatter(proj_up, "dp", scatter_dimension=1, tiled=True)
+    cot_later, proj_up = lax.optimization_barrier((cotangent, proj_up))
+    cot_all = spread_quarter(cot_later)
     projected = proj_up[:n_proj].astype(jnp.bfloat16).reshape(3, head_slice, HEADS, ROWS)
     up_input = proj_up[n_proj:]
     activated, gelu_slope = gelu_pair(up_input)
@@ -224,7 +235,7 @@
     branch = lax.dot_general(
         head_rows_all, head_flat, contract_rows, preferred_element_type=jnp.float32
     ) + lax.dot_general(up_output_all, down_weight, contract_rows, preferred_element_type=jnp.float32)
-    branch_local = gather_quarter(branch, rows)
+    branch_local = gather_quarter_exchange(branch, rows)
     mixed = (widened + branch_local).astype(jnp.bfloat16)
 
     down_grad = blockwise_grad(up_output_all, cot_all, n_dp)

time: 564 us -> 583 us (1.034)
  waiting for transfers between devices: 262 us -> 244 us
  blocking collectives: 69.5 us -> 87.1 us
  local copies, waits for them, and re-layouts: 71.5 us -> 81.5 us
  matrix products: 75.4 us -> 83.1 us
    all_gather x2, waiting for transfers between devices: 58.2 us -> 106 us  [spread_quarter(): pieces = lax.all_gather(swap(block), 'mp', axis=0, tiled=False)]
    reduce_scatter x1, waiting for transfers between devices: 33.3 us -> 0.01 us  [shards(): back = lax.psum_scatter(back, 'dp', scatter_dimension=1, tiled=True)]
    reduce_scatter x2 -> x1, waiting for transfers between devices: 108 us -> 77.5 us  [gather_quarter(): summed = lax.psum_scatter(pieces, 'mp', scatter_dimension=0, tiled=True)]
    all_to_all x1 -> x2, blocking collectives: 11 us -> 26 us  [the longest x1 13.7 us: shards(): lax.all_to_all(projected, 'mp', split_axis=2, concat_axis=1, tiled=True)]
    psum x1, blocking collectives: 6.85 us -> 19.2 us  [shards(): gain_grad = lax.psum(gain_piece, 'dp')]
    slice x10, local copies, waits for them, and re-layouts: 10.8 us -> 20.6 us  [blockwise_grad(): right[block * rows:(block + 1) * rows]]
    reshape x0 -> x2, local copies, waits for them, and re-layouts: none -> 9.06 us  [gather_quarter_exchange(): pieces = partial.reshape(n_dp, rows, ratio, width)]
    all_gather x1, blocking collectives: 31 us -> 22.2 us  [shards(): lax.all_gather(jnp.stack([block_mean, block_m2]), 'mp', axis=0, tiled=False)]
  transfers between devices with their start and end apart: 15 -> 14, of which waited for: 9 -> 6; matrix products, arithmetic and copies ran while one was open for 23% -> 29% of each run, Pallas kernels for 0% -> 0%
where the time goes in v3:
time: 583 us; the launch traced here: 572 us
  waiting for transfers between devices  244 us (42%)
  blocking collectives  87.1 us (15%)
  matrix products  83.1 us (14%)
  local copies, waits for them, and re-layouts  81.5 us (14%)
  other arithmetic  35.2 us (6%)
  starting transfers between devices  26.2 us (4%)
  between operations  15.2 us (3%)
    all_gather x2, waiting for transfers between devices, spread_quarter(): pieces = lax.all_gather(swap(block), 'mp', axis=0, tiled=False)  106 us
    reduce_scatter x1, waiting for transfers between devices, gather_quarter(): summed = lax.psum_scatter(pieces, 'mp', scatter_dimension=0, tiled=True)  77.5 us
    reduce_scatter x1, waiting for transfers between devices, shards(): proj_up = lax.psum_scatter(proj_up, 'dp', scatter_dimension=1, tiled=True)  52 us
    dot_general x16, matrix products, blockwise_grad(): jnp.dot(left[:, block * rows:(block + 1) * rows], right[block * rows:(blo...  40 us
    all_gather x1, blocking collectives, shards(): lax.all_gather(jnp.stack([block_mean, block_m2]), 'mp', axis=0, tiled=False)  22.2 us
    slice x10, local copies, waits for them, and re-layouts, blockwise_grad(): right[block * rows:(block + 1) * rows]  20.6 us
    psum x1, blocking collectives, shards(): lax.psum((jnp.sum(scaled, axis=1), jnp.sum(scaled * normed, axis=1)), 'mp')  19.6 us
    psum x1, blocking collectives, shards(): gain_grad = lax.psum(gain_piece, 'dp')  19.2 us
  transfers between devices with their start and end apart: 14, of which 6 were waited for; matrix products, arithmetic and copies ran while one was open for 29% of the time, Pallas kernels for 0%

profile of v3, /device:TPU:0, one launch (start us, length us, event | category | flops | bytes accessed | tf_op | source)
XLA Modules:
  0.0 572.0 jit_solution(8908509453695608624)
XLA Ops:
  10.3 22.2 %all-gather.3 = f32[8,2,128]{2,1,0:T(2,128)S(1)} all-gather(f32[1,2,128]{2,1,0:T(2,128)S(1)} %maximum_bitcast_fusion), channel_id=2, replica_groups=mesh['dp'=4,'mp'=8] {'mp'}, dimensions={0}, use_global_device_ids=true | all-gather | bytes 9216 | tf_op jit(solution)/shard_map/all_gather | solution.py:180
  35.1 50.5 %all-gather.13.cloned.1.call-done = bf16[1024,768]{1,0:T(8,128)(2,1)} async-done(((bf16[128,768]{1,0:T(8,128)(2,1)}), bf16[1024,768]{1,0:T(8,128)(2,1)}) %all-gather.13.cloned.1.call-update) | async-done | bytes 1572880 | tf_op jit(solution)/shard_map/all_gather | solution.py:130
  85.6 3.0 copy.97
  91.2 2.6 convolution_bitcast_fusion.1
  93.8 2.7 pad_maximum_fusion
  96.6 52.0 %reduce-scatter.4.cloned.1.call-done = f32[2688,128]{0,1:T(8,128)} async-done(((f32[2688,512]{0,1:T(8,128)}), f32[2688,128]{0,1:T(8,128)}) %reduce-scatter.4.cloned.1.call-update) | async-done | bytes 1376272 | tf_op jit(solution)/shard_map/reduce_scatter | solution.py:198
  148.7 3.0 collective-permute-start.2
  151.7 55.3 %all-gather.15.cloned.1.call-done = bf16[1024,768]{1,0:T(8,128)(2,1)} async-done(((bf16[128,768]{1,0:T(8,128)(2,1)}), bf16[1024,768]{1,0:T(8,128)(2,1)}) %all-gather.15.cloned.1.call-update) | async-done | bytes 1572880 | tf_op jit(solution)/shard_map/all_gather | solution.py:130
  207.0 3.2 copy.109
  211.5 2.6 convolution_bitcast_fusion
  221.1 13.7 %all_to_all.65 = bf16[3,16,24,128]{3,1,0,2:T(8,128)(2,1)S(1)} all-to-all(bf16[3,16,24,128]{3,1,0,2:T(8,128)(2,1)S(1)} %copy.99), channel_id=1, replica_groups=mesh['dp'=4,'mp'=8] {'mp'}, dimensions={2} | all-to-all | bytes 589824 | tf_op jit(solution)/shard_map/all_to_all | solution.py:209
  240.8 2.5 copy.103
  243.4 2.5 reshape.211
  250.1 2.5 convolution_convert_fusion.17
  254.2 4.0 all-to-all-start.1
  260.1 5.5 all-to-all-done.1
  275.3 4.0 all-to-all-start.3
  279.3 2.5 fusion.44
  283.6 2.8 all-to-all-done.3
  288.5 2.3 reshape.204
  293.1 3.3 fusion.102
  300.7 4.2 bitcast_reduce_fusion
  306.2 2.4 convolution_convert_fusion.16
  311.4 12.3 %all_to_all.66 = bf16[3,128,3,128]{3,2,0,1:T(4,128)(2,1)S(1)} all-to-all(bf16[3,128,3,128]{3,2,0,1:T(4,128)(2,1)S(1)} %copy.115), channel_id=1, replica_groups=mesh['dp'=4,'mp'=8] {'mp'}, dimensions={1} | all-to-all | bytes 589824 | tf_op jit(solution)/shard_map/all_to_all | solution.py:264
  330.6 2.5 fusion.104
  340.9 2.5 fusion.103
  351.1 5.0 fusion.29
  356.2 3.6 convolution_add_fusion
  359.8 5.2 reshape.199
  365.0 3.9 copy.108
  368.9 4.5 all-to-all-start.2
  373.6 3.0 fusion.16
  376.6 2.8 fusion.15
  379.4 3.6 fusion.31
  383.0 6.7 %convolution_add_fusion.1 = f32[512,1536]{1,0:T(8,128)} fusion(f32[512,1536]{1,0:T(8,128)S(1)} %fusion.31, bf16[1536,1536]{1,0:T(8,128)(2,1)} %param.11, bf16[2688,512]{0,1:T(8,128)(2,1)S(1)} %copy-done.6), kind=kOutput, calls=%fused_computation.29 | convolution fusion | flops 2416705536 | bytes 12582912 | tf_op jit(solution)/shard_map/dot_general | solution.py:286
  389.7 3.8 reshape.206
  403.2 2.5 fusion.13
  405.7 5.3 add_convert_fusion
  417.6 4.0 fusion.5
  421.6 3.9 add_convert_fusion.1
  425.5 77.5 %reduce-scatter.8.cloned.1.call-done = f32[1,128,768]{2,1,0:T(8,128)} async-done(((f32[8,128,768]{2,1,0:T(8,128)}), f32[1,128,768]{2,1,0:T(8,128)}) %reduce-scatter.8.cloned.1.call-update) | async-done | bytes 393232 | tf_op jit(solution)/shard_map/reduce_scatter | solution.py:141
  503.0 4.5 collective-permute-start.3
  507.4 6.3 %fusion.3 = bf16[1152,1536]{1,0:T(8,128)(2,1)} fusion(f32[1152,1536]{1,0:T(8,128)} %fusion.5, bf16[128,1536]{0,1:T(8,128)(2,1)} %bitcast.173, bf16[2688,512]{0,1:T(8,128)(2,1)} %all-gather.11.cloned.1.call-done), kind=kOutput, calls=%fused_computation.6 | convolution fusion | flops 460062720 | bytes 11304960 | tf_op jit(solution)/shard_map/dot_general | solution.py:159
  513.7 2.8 reduce_sum.193
  516.6 4.5 collective-permute-start.1
  522.9 19.2 %psum.23 = f32[768]{0:T(1024)} all-reduce(f32[768]{0:T(1024)S(1)} %get-tuple-element.13), channel_id=1, replica_groups=mesh['dp'=4,'mp'=8] {'dp'}, use_global_device_ids=true, to_apply=%region_25.0 | all-reduce | flops 768 | bytes 6144 | tf_op jit(solution)/shard_map/psum | solution.py:298
  542.2 19.6 %all-reduce = (f32[128]{0:T(128)}, f32[128]{0:T(128)S(1)}) all-reduce(f32[128]{0:T(128)} %get-tuple-element.14, f32[128]{0:T(128)} %get-tuple-element.15), channel_id=1, replica_groups=mesh['dp'=4,'mp'=8] {'mp'}, use_global_device_ids=true, to_apply=%region_23.0 | all-reduce | flops 256 | bytes 2048 | tf_op jit(solution)/shard_map/psum | solution.py:290
  562.5 2.3 fusion.59
  (175 shorter events, 95.7 us)
Async XLA Ops:
  7.2 81.7 %copy-start = (bf16[3,16,24,1536]{3,2,1,0:T(8,128)(2,1)S(1)}, bf16[3,16,24,1536]{3,2,1,0:T(8,128)(2,1)}, u32[]{:S(2)}) copy-start(bf16[3,16,24,1536]{3,2,1,0:T(8,128)(2,1)} %param.9) | copy-start | bytes 10616836
  7.2 78.4 %all-gather.13.cloned.1.call-start = ((), (), s32[]{:S(2)}) async-start(), calls=%async_computation.13 | async-start | bytes 1769472 | tf_op jit(solution)/shard_map/all_gather | solution.py:130
  32.5 2.5 copy-start.26
  32.6 2.4 copy-start.28
  33.7 1.3 collective-permute-start
  35.0 113.6 %reduce-scatter.4.cloned.1.call-start = ((), (), s32[]{:S(2)}) async-start(), calls=%async_computation.8 | async-start | bytes 6881280 | tf_op jit(solution)/shard_map/reduce_scatter | solution.py:198
  88.6 2.5 slice-start.2
  88.9 2.3 slice-start.3
  96.6 110.4 %all-gather.15.cloned.1.call-start = ((), (), s32[]{:S(2)}) async-start(), calls=%async_computation.14 | async-start | bytes 1769472 | tf_op jit(solution)/shard_map/all_gather | solution.py:130
  148.7 3.0 collective-permute-start.2
  151.7 118.8 %reduce-scatter.6.cloned.1.call-start = ((), (), s32[]{:S(2)}) async-start(), calls=%async_computation.10 | async-start | bytes 4915200 | tf_op jit(solution)/shard_map/reduce_scatter | solution.py:250
  207.0 3.5 copy-start.19
  207.0 4.5 slice-start
  210.2 1.3 slice-start.1
  234.8 0.7 copy-start.18
  245.9 3.1 copy-start.21
  245.9 3.1 copy-start.24
  245.9 3.1 copy-start.25
  247.2 1.1 copy-start.2
  248.4 0.6 copy-start.23
  254.2 11.4 %all-to-all-start.1 = ((bf16[128,3,128]{2,1,0:T(4,128)(2,1)}), bf16[128,3,128]{2,1,0:T(4,128)(2,1)}, u32[]{:S(2)}, u32[]{:S(2)}) async-start(bf16[128,3,128]{2,1,0:T(4,128)(2,1)} %copy.104), calls=%async_computation.2 | async-start | bytes 262144 | tf_op jit(solution)/shard_map/all_to_all | solution.py:216
  275.3 11.1 %all-to-all-start.3 = ((bf16[16,24,128]{2,0,1:T(8,128)(2,1)}), bf16[16,24,128]{2,0,1:T(8,128)(2,1)}, u32[]{:S(2)}, u32[]{:S(2)}) async-start(bf16[16,24,128]{2,0,1:T(8,128)(2,1)} %copy.112), calls=%async_computation.5 | async-start | bytes 196608 | tf_op jit(solution)/shard_map/all_to_all | solution.py:254
  279.3 71.9 %all-gather.9.cloned.1.call-start = ((), (), s32[]{:S(2)}) async-start(), calls=%async_computation.9 | async-start | bytes 2457600 | tf_op jit(solution)/shard_map/all_gather | solution.py:231
  283.5 95.9 %all-gather.11.cloned.1.call-start = ((), (), s32[]{:S(2)}) async-start(), calls=%async_computation.11 | async-start | bytes 3440640 | tf_op jit(solution)/shard_map/all_gather | solution.py:278
  308.6 2.2 copy-start.17
  308.6 2.5 copy-start.22
  351.1 5.0 copy-start.20
  368.9 144.8 %all-to-all-start.2 = ((f32[8,128,768]{2,1,0:T(8,128)}), f32[8,128,768]{2,1,0:T(8,128)}, u32[]{:S(2)}, u32[]{:S(2)}) async-start(f32[8,128,768]{2,1,0:T(8,128)} %bitcast.164), calls=%async_computation.3 | async-start | bytes 6291456 | tf_op jit(solution)/shard_map/all_to_all | solution.py:151
  373.3 129.6 %reduce-scatter.8.cloned.1.call-start = ((), (), s32[]{:S(2)}) async-start(), calls=%async_computation.12 | async-start | bytes 3538944 | tf_op jit(solution)/shard_map/reduce_scatter | solution.py:141
  373.6 3.0 copy-start.11
  379.4 3.6 copy-start.6
  395.5 1.5 copy-start.5
  395.5 1.6 copy-start.12
  397.1 1.4 copy-start.9
  398.5 1.4 copy-start.10
  400.0 3.0 copy-start.4
  401.4 1.8 copy-start.3
  401.4 1.8 copy-start.16
  405.7 5.3 copy-start.7
  405.7 5.3 copy-start.8
  411.0 1.4 copy-start.13
  412.5 1.4 copy-start.15
  413.9 1.4 copy-start.14
  503.0 18.1 %collective-permute-start.3 = (f32[128,768]{1,0:T(8,128)}, f32[128,768]{1,0:T(8,128)}, u32[]{:S(2)}, u32[]{:S(2)}) collective-permute-start(f32[128,768]{1,0:T(8,128)} %bitcast.216), channel_id=1, source_target_pairs={{0,0},{1,1},{2,8},{3,9},{4,16},{5,17},{6,24},{7,25},{8,2},{9,3},{1... | collective-permute-start | bytes 1179656 | tf_op jit(solution)/shard_map/ppermute | solution.py:123
  507.4 57.3 %copy-start.1 = (bf16[3,16,24,1536]{3,2,1,0:T(8,128)(2,1)S(1)}, bf16[3,16,24,1536]{3,2,1,0:T(8,128)(2,1)}, u32[]{:S(2)}) copy-start(bf16[3,16,24,1536]{3,2,1,0:T(8,128)(2,1)} %param.9) | copy-start | bytes 10616836
  513.7 7.3 %copy-start.27 = (f32[128]{0:T(128)S(1)}, f32[128]{0:T(128)}, u32[]{:S(2)}) copy-start(f32[128]{0:T(128)} %copy-done.26) | copy-start | bytes 1540
  513.7 7.3 %copy-start.29 = (f32[128]{0:T(128)S(1)}, f32[128]{0:T(128)}, u32[]{:S(2)}) copy-start(f32[128]{0:T(128)} %copy-done.28) | copy-start | bytes 1540
  516.6 45.9 %collective-permute-start.1 = (f32[128,768]{1,0:T(8,128)}, f32[128,768]{1,0:T(8,128)}, u32[]{:S(2)}, u32[]{:S(2)}) collective-permute-start(f32[128,768]{1,0:T(8,128)} %reduce_sum.193), channel_id=1, source_target_pairs={{0,0},{1,1},{2,8},{3,9},{4,16},{5,17},{6,24},{7,25},{8,2},{9,3},{1... | collective-permute-start | bytes 1179656 | tf_op jit(solution)/shard_map/ppermute | solution.py:123
Sparse Core Ops, SparseCore 0:
  35.2 50.3 all-gather.12
  96.7 51.9 reduce-scatter.3
  151.8 55.1 all-gather.14
  216.4 41.6 reduce-scatter.5
  283.7 23.1 all-gather.8
  330.7 24.8 all-gather.10
  395.7 107.2 reduce-scatter.7

commit v4 on v3

--- a/solution.py
+++ b/solution.py
@@ -186,6 +186,7 @@
     gain_wide = norm_gain.astype(jnp.float32)
     hidden_local = (normed * gain_wide).astype(jnp.bfloat16)
     hidden_all = spread_quarter(hidden_local)
+    cot_all = spread_quarter(cotangent)
 
     n_proj = qkv_flat.shape[0]
     proj_up = jnp.concatenate(
@@ -196,8 +197,7 @@
         axis=0,
     )
     proj_up = lax.psum_scatter(proj_up, "dp", scatter_dimension=1, tiled=True)
-    cot_later, proj_up = lax.optimization_barrier((cotangent, proj_up))
-    cot_all = spread_quarter(cot_later)
+    cot_later, proj_up = lax.optimization_barrier((cot_all, proj_up))
     projected = proj_up[:n_proj].astype(jnp.bfloat16).reshape(3, head_slice, HEADS, ROWS)
     up_input = proj_up[n_proj:]
     activated, gelu_slope = gelu_pair(up_input)
@@ -242,8 +242,8 @@
     head_grad = blockwise_grad(head_rows_all, cot_all, n_dp)
     back = jnp.concatenate(
         [
-            lax.dot_general(head_flat, cot_all, contract_cols, preferred_element_type=jnp.float32),
-            lax.dot_general(down_weight, cot_all, contract_cols, preferred_element_type=jnp.float32),
+            lax.dot_general(head_flat, cot_later, contract_cols, preferred_element_type=jnp.float32),
+            lax.dot_general(down_weight, cot_later, contract_cols, preferred_element_type=jnp.float32),
         ],
         axis=0,
     )

time: 583 us -> 564 us (0.967)
  waiting for transfers between devices: 244 us -> 219 us
    all_gather x2, waiting for transfers between devices: 106 us -> 83.8 us  [spread_quarter(): pieces = lax.all_gather(swap(block), 'mp', axis=0, tiled=False)]
  transfers between devices with their start and end apart: 14 -> 14, of which waited for: 6 -> 6; matrix products, arithmetic and copies ran while one was open for 29% -> 32% of each run, Pallas kernels for 0% -> 0%
where the time goes in v4:
time: 564 us; the launch traced here: 554 us
  waiting for transfers between devices  219 us (39%)
  blocking collectives  89.5 us (16%)
  matrix products  86.8 us (15%)
  local copies, waits for them, and re-layouts  82.3 us (15%)
  other arithmetic  35.3 us (6%)
  starting transfers between devices  26.2 us (5%)
  between operations  15.1 us (3%)
    all_gather x2, waiting for transfers between devices, spread_quarter(): pieces = lax.all_gather(swap(block), 'mp', axis=0, tiled=False)  83.8 us
    reduce_scatter x1, waiting for transfers between devices, gather_quarter(): summed = lax.psum_scatter(pieces, 'mp', scatter_dimension=0, tiled=True)  76.6 us
    reduce_scatter x1, waiting for transfers between devices, shards(): proj_up = lax.psum_scatter(proj_up, 'dp', scatter_dimension=1, tiled=True)  50.1 us
    dot_general x16, matrix products, blockwise_grad(): jnp.dot(left[:, block * rows:(block + 1) * rows], right[block * rows:(blo...  40 us
    all_gather x1, blocking collectives, shards(): lax.all_gather(jnp.stack([block_mean, block_m2]), 'mp', axis=0, tiled=False)  22.2 us
    slice x10, local copies, waits for them, and re-layouts, blockwise_grad(): right[block * rows:(block + 1) * rows]  20.4 us
    psum x1, blocking collectives, shards(): lax.psum((jnp.sum(scaled, axis=1), jnp.sum(scaled * normed, axis=1)), 'mp')  19.8 us
    psum x1, blocking collectives, shards(): gain_grad = lax.psum(gain_piece, 'dp')  19.3 us
  transfers between devices with their start and end apart: 14, of which 6 were waited for; matrix products, arithmetic and copies ran while one was open for 32% of the time, Pallas kernels for 0%

profile of v4, /device:TPU:0, one launch (start us, length us, event | category | flops | bytes accessed | tf_op | source)
XLA Modules:
  0.0 554.1 jit_solution(10770902385613330191)
XLA Ops:
  10.3 22.2 %all-gather.3 = f32[8,2,128]{2,1,0:T(2,128)S(1)} all-gather(f32[1,2,128]{2,1,0:T(2,128)S(1)} %maximum_bitcast_fusion), channel_id=3, replica_groups=mesh['dp'=4,'mp'=8] {'mp'}, dimensions={0}, use_global_device_ids=true | all-gather | bytes 9216 | tf_op jit(solution)/shard_map/all_gather | solution.py:180
  35.1 3.0 collective-permute-start
  38.2 49.6 %all-gather.15.cloned.1.call-done = bf16[1024,768]{1,0:T(8,128)(2,1)} async-done(((bf16[128,768]{1,0:T(8,128)(2,1)}), bf16[1024,768]{1,0:T(8,128)(2,1)}) %all-gather.15.cloned.1.call-update) | async-done | bytes 1572880 | tf_op jit(solution)/shard_map/all_gather | solution.py:130
  87.7 3.0 copy.98
  93.3 2.6 convolution_bitcast_fusion.1
  96.0 2.7 pad_maximum_fusion
  98.8 34.2 %all-gather.13.cloned.1.call-done = bf16[1024,768]{1,0:T(8,128)(2,1)} async-done(((bf16[128,768]{1,0:T(8,128)(2,1)}), bf16[1024,768]{1,0:T(8,128)(2,1)}) %all-gather.13.cloned.1.call-update) | async-done | bytes 1572880 | tf_op jit(solution)/shard_map/all_gather | solution.py:130
  133.0 3.0 copy.97
  137.4 50.1 %reduce-scatter.4.cloned.1.call-done = f32[2688,128]{0,1:T(8,128)} async-done(((f32[2688,512]{0,1:T(8,128)}), f32[2688,128]{0,1:T(8,128)}) %reduce-scatter.4.cloned.1.call-update) | async-done | bytes 1376272 | tf_op jit(solution)/shard_map/reduce_scatter | solution.py:199
  187.5 2.9 convolution_bitcast_fusion.3
  190.3 4.5 convolution_bitcast_fusion
  201.8 15.8 %all_to_all.65 = bf16[3,16,24,128]{3,1,0,2:T(8,128)(2,1)S(1)} all-to-all(bf16[3,16,24,128]{3,1,0,2:T(8,128)(2,1)S(1)} %copy.100), channel_id=1, replica_groups=mesh['dp'=4,'mp'=8] {'mp'}, dimensions={2} | all-to-all | bytes 589824 | tf_op jit(solution)/shard_map/all_to_all | solution.py:209
  223.7 2.6 copy.104
  226.2 2.5 reshape.211
  232.9 2.5 convolution_convert_fusion.17
  237.1 4.0 all-to-all-start.1
  242.9 5.5 all-to-all-done.1
  258.1 4.0 all-to-all-start.3
  262.1 2.5 fusion.44
  266.4 2.8 all-to-all-done.3
  271.4 2.3 reshape.204
  275.9 3.3 fusion.102
  283.5 4.2 bitcast_reduce_fusion
  289.0 2.4 convolution_convert_fusion.16
  294.2 12.4 %all_to_all.66 = bf16[3,128,3,128]{3,2,0,1:T(4,128)(2,1)S(1)} all-to-all(bf16[3,128,3,128]{3,2,0,1:T(4,128)(2,1)S(1)} %copy.115), channel_id=1, replica_groups=mesh['dp'=4,'mp'=8] {'mp'}, dimensions={1} | all-to-all | bytes 589824 | tf_op jit(solution)/shard_map/all_to_all | solution.py:264
  313.4 2.5 fusion.103
  323.7 2.5 fusion.104
  333.9 5.0 fusion.29
  338.9 3.7 convolution_add_fusion
  342.6 5.2 reshape.201
  347.7 3.9 copy.109
  351.6 4.5 all-to-all-start.2
  356.4 3.0 fusion.16
  359.4 2.8 fusion.15
  362.2 3.6 fusion.31
  365.8 6.7 %convolution_add_fusion.1 = f32[512,1536]{1,0:T(8,128)} fusion(f32[512,1536]{1,0:T(8,128)S(1)} %fusion.31, bf16[1536,1536]{1,0:T(8,128)(2,1)} %param.11, bf16[2688,512]{0,1:T(8,128)(2,1)S(1)} %copy-done.6), kind=kOutput, calls=%fused_computation.29 | convolution fusion | flops 2416705536 | bytes 12582912 | tf_op jit(solution)/shard_map/dot_general | solution.py:286
  372.5 3.8 reshape.206
  386.0 2.5 fusion.13
  388.5 5.3 add_convert_fusion
  400.3 4.0 fusion.5
  404.4 3.9 add_convert_fusion.1
  408.3 76.6 %reduce-scatter.8.cloned.1.call-done = f32[1,128,768]{2,1,0:T(8,128)} async-done(((f32[8,128,768]{2,1,0:T(8,128)}), f32[1,128,768]{2,1,0:T(8,128)}) %reduce-scatter.8.cloned.1.call-update) | async-done | bytes 393232 | tf_op jit(solution)/shard_map/reduce_scatter | solution.py:141
  484.9 4.5 collective-permute-start.3
  489.3 6.3 %fusion.3 = bf16[1152,1536]{1,0:T(8,128)(2,1)} fusion(f32[1152,1536]{1,0:T(8,128)} %fusion.5, bf16[128,1536]{0,1:T(8,128)(2,1)} %bitcast.173, bf16[2688,512]{0,1:T(8,128)(2,1)} %all-gather.11.cloned.1.call-done), kind=kOutput, calls=%fused_computation.6 | convolution fusion | flops 460062720 | bytes 11304960 | tf_op jit(solution)/shard_map/dot_general | solution.py:159
  495.6 2.8 reduce_sum.193
  498.5 4.5 collective-permute-start.2
  504.8 19.3 %psum.23 = f32[768]{0:T(1024)} all-reduce(f32[768]{0:T(1024)S(1)} %get-tuple-element.13), channel_id=1, replica_groups=mesh['dp'=4,'mp'=8] {'dp'}, use_global_device_ids=true, to_apply=%region_25.0 | all-reduce | flops 768 | bytes 6144 | tf_op jit(solution)/shard_map/psum | solution.py:298
  524.1 19.8 %all-reduce = (f32[128]{0:T(128)}, f32[128]{0:T(128)S(1)}) all-reduce(f32[128]{0:T(128)} %get-tuple-element.14, f32[128]{0:T(128)} %get-tuple-element.15), channel_id=1, replica_groups=mesh['dp'=4,'mp'=8] {'mp'}, use_global_device_ids=true, to_apply=%region_23.0 | all-reduce | flops 256 | bytes 2048 | tf_op jit(solution)/shard_map/psum | solution.py:290
  (170 shorter events, 97.9 us)
Async XLA Ops:
  7.2 83.9 %copy-start = (bf16[3,16,24,1536]{3,2,1,0:T(8,128)(2,1)S(1)}, bf16[3,16,24,1536]{3,2,1,0:T(8,128)(2,1)}, u32[]{:S(2)}) copy-start(bf16[3,16,24,1536]{3,2,1,0:T(8,128)(2,1)} %param.9) | copy-start | bytes 10616836
  7.2 80.6 %all-gather.15.cloned.1.call-start = ((), (), s32[]{:S(2)}) async-start(), calls=%async_computation.14 | async-start | bytes 1769472 | tf_op jit(solution)/shard_map/all_gather | solution.py:130
  32.5 2.5 copy-start.26
  32.6 2.5 copy-start.28
  33.7 1.4 collective-permute-start.1
  35.0 97.9 %all-gather.13.cloned.1.call-start = ((), (), s32[]{:S(2)}) async-start(), calls=%async_computation.13 | async-start | bytes 1769472 | tf_op jit(solution)/shard_map/all_gather | solution.py:130
  35.1 3.0 collective-permute-start
  38.1 149.4 %reduce-scatter.4.cloned.1.call-start = ((), (), s32[]{:S(2)}) async-start(), calls=%async_computation.8 | async-start | bytes 6881280 | tf_op jit(solution)/shard_map/reduce_scatter | solution.py:199
  90.8 2.5 slice-start
  91.1 2.3 slice-start.1
  98.7 154.6 %reduce-scatter.6.cloned.1.call-start = ((), (), s32[]{:S(2)}) async-start(), calls=%async_computation.10 | async-start | bytes 4915200 | tf_op jit(solution)/shard_map/reduce_scatter | solution.py:250
  187.5 2.9 copy-start.19
  217.6 0.7 copy-start.18
  228.7 3.1 copy-start.21
  228.7 3.1 copy-start.24
  228.7 3.1 copy-start.25
  230.1 1.1 copy-start.2
  231.2 0.6 copy-start.23
  237.1 11.4 %all-to-all-start.1 = ((bf16[128,3,128]{2,1,0:T(4,128)(2,1)}), bf16[128,3,128]{2,1,0:T(4,128)(2,1)}, u32[]{:S(2)}, u32[]{:S(2)}) async-start(bf16[128,3,128]{2,1,0:T(4,128)(2,1)} %copy.105), calls=%async_computation.2 | async-start | bytes 262144 | tf_op jit(solution)/shard_map/all_to_all | solution.py:216
  258.1 11.1 %all-to-all-start.3 = ((bf16[16,24,128]{2,0,1:T(8,128)(2,1)}), bf16[16,24,128]{2,0,1:T(8,128)(2,1)}, u32[]{:S(2)}, u32[]{:S(2)}) async-start(bf16[16,24,128]{2,0,1:T(8,128)(2,1)} %copy.112), calls=%async_computation.5 | async-start | bytes 196608 | tf_op jit(solution)/shard_map/all_to_all | solution.py:254
  262.1 71.8 %all-gather.9.cloned.1.call-start = ((), (), s32[]{:S(2)}) async-start(), calls=%async_computation.9 | async-start | bytes 2457600 | tf_op jit(solution)/shard_map/all_gather | solution.py:231
  266.4 95.8 %all-gather.11.cloned.1.call-start = ((), (), s32[]{:S(2)}) async-start(), calls=%async_computation.11 | async-start | bytes 3440640 | tf_op jit(solution)/shard_map/all_gather | solution.py:278
  291.4 2.2 copy-start.17
  291.4 2.5 copy-start.22
  333.9 5.1 copy-start.20
  351.6 144.0 %all-to-all-start.2 = ((f32[8,128,768]{2,1,0:T(8,128)}), f32[8,128,768]{2,1,0:T(8,128)}, u32[]{:S(2)}, u32[]{:S(2)}) async-start(f32[8,128,768]{2,1,0:T(8,128)} %bitcast.164), calls=%async_computation.3 | async-start | bytes 6291456 | tf_op jit(solution)/shard_map/all_to_all | solution.py:151
  356.1 128.7 %reduce-scatter.8.cloned.1.call-start = ((), (), s32[]{:S(2)}) async-start(), calls=%async_computation.12 | async-start | bytes 3538944 | tf_op jit(solution)/shard_map/reduce_scatter | solution.py:141
  356.4 3.0 copy-start.11
  362.2 3.6 copy-start.6
  378.3 1.5 copy-start.5
  378.3 1.6 copy-start.12
  379.9 1.4 copy-start.9
  381.3 1.4 copy-start.10
  382.7 3.0 copy-start.4
  384.2 1.8 copy-start.3
  384.2 1.8 copy-start.13
  388.5 5.3 copy-start.7
  388.5 5.3 copy-start.8
  393.8 1.4 copy-start.14
  395.2 1.4 copy-start.16
  396.7 1.4 copy-start.15
  484.9 18.1 %collective-permute-start.3 = (f32[128,768]{1,0:T(8,128)}, f32[128,768]{1,0:T(8,128)}, u32[]{:S(2)}, u32[]{:S(2)}) collective-permute-start(f32[128,768]{1,0:T(8,128)} %bitcast.214), channel_id=1, source_target_pairs={{0,0},{1,1},{2,8},{3,9},{4,16},{5,17},{6,24},{7,25},{8,2},{9,3},{1... | collective-permute-start | bytes 1179656 | tf_op jit(solution)/shard_map/ppermute | solution.py:123
  489.3 57.5 %copy-start.1 = (bf16[3,16,24,1536]{3,2,1,0:T(8,128)(2,1)S(1)}, bf16[3,16,24,1536]{3,2,1,0:T(8,128)(2,1)}, u32[]{:S(2)}) copy-start(bf16[3,16,24,1536]{3,2,1,0:T(8,128)(2,1)} %param.9) | copy-start | bytes 10616836
  495.6 7.3 %copy-start.27 = (f32[128]{0:T(128)S(1)}, f32[128]{0:T(128)}, u32[]{:S(2)}) copy-start(f32[128]{0:T(128)} %copy-done.26) | copy-start | bytes 1540
  495.6 7.3 %copy-start.29 = (f32[128]{0:T(128)S(1)}, f32[128]{0:T(128)}, u32[]{:S(2)}) copy-start(f32[128]{0:T(128)} %copy-done.28) | copy-start | bytes 1540
  498.5 46.1 %collective-permute-start.2 = (f32[128,768]{1,0:T(8,128)}, f32[128,768]{1,0:T(8,128)}, u32[]{:S(2)}, u32[]{:S(2)}) collective-permute-start(f32[128,768]{1,0:T(8,128)} %reduce_sum.193), channel_id=1, source_target_pairs={{0,0},{1,1},{2,8},{3,9},{4,16},{5,17},{6,24},{7,25},{8,2},{9,3},{1... | collective-permute-start | bytes 1179656 | tf_op jit(solution)/shard_map/ppermute | solution.py:123
Sparse Core Ops, SparseCore 0:
  35.2 52.5 all-gather.14
  89.9 42.9 all-gather.12
  135.5 51.9 reduce-scatter.3
  197.2 42.8 reduce-scatter.5
  266.5 22.2 all-gather.8
  313.6 23.8 all-gather.10
  378.4 106.3 reduce-scatter.7

commit v5 on v4

--- a/solution.py
+++ b/solution.py
@@ -127,7 +127,8 @@
     n_dp, n_mp = lax.axis_size("dp"), lax.axis_size("mp")
     ratio = n_mp // n_dp
     rows, width = block.shape
-    pieces = lax.all_gather(swap(block), "mp", axis=0, tiled=False)
+    copies = jnp.broadcast_to(swap(block)[None], (n_mp, rows, width))
+    pieces = lax.all_to_all(copies, "mp", split_axis=0, concat_axis=0, tiled=True)
     pieces = pieces.reshape(n_dp, ratio, rows, width)
     return jnp.transpose(pieces, (0, 2, 1, 3)).reshape(n_dp * rows, ratio * width)
 
@@ -284,7 +285,7 @@
     input_partial = lax.dot_general(
         proj_grad_all, qkv_flat, contract_rows, preferred_element_type=jnp.float32
     ) + lax.dot_general(up_upstream_all, up_weight, contract_rows, preferred_element_type=jnp.float32)
-    input_local = gather_quarter(input_partial, rows)
+    input_local = gather_quarter_exchange(input_partial, rows)
 
     scaled = input_local * gain_wide
     plain_sum, cross_sum = lax.psum(

time: 564 us -> 546 us (0.968)
  waiting for transfers between devices: 219 us -> 109 us
  blocking collectives: 89.5 us -> 174 us
  local copies, waits for them, and re-layouts: 82.3 us -> 74 us
  starting transfers between devices: 26.2 us -> 34 us
    all_to_all x1 -> x3, blocking collectives: 12.4 us -> 107 us  [the longest x2 96.3 us: spread_quarter(): lax.all_to_all(copies, 'mp', split_axis=0, concat_axis=0, tiled=True)]
    all_to_all x1 -> x2, waiting for transfers between devices: 0.01 us -> 85.6 us  [gather_quarter_exchange(): lax.all_to_all(pieces, 'mp', split_axis=0, concat_axis=0, tiled=True)]
    all_gather x2 -> x0, waiting for transfers between devices: 83.8 us -> none  [spread_quarter(): pieces = lax.all_gather(swap(block), 'mp', axis=0, tiled=False)]
    reduce_scatter x1 -> x0, waiting for transfers between devices: 76.6 us -> none  [gather_quarter(): summed = lax.psum_scatter(pieces, 'mp', scatter_dimension=0, tiled=True)]
    reduce_scatter x1, waiting for transfers between devices: 50.1 us -> 0.01 us  [shards(): proj_up = lax.psum_scatter(proj_up, 'dp', scatter_dimension=1, tiled=True)]
    slice x10 -> x2, local copies, waits for them, and re-layouts: 20.4 us -> 2.25 us  [blockwise_grad(): right[block * rows:(block + 1) * rows]]
    psum x1, blocking collectives: 19.3 us -> 10.9 us  [shards(): gain_grad = lax.psum(gain_piece, 'dp')]
    reduce_scatter x1, waiting for transfers between devices: 0.01 us -> 6.92 us  [shards(): back = lax.psum_scatter(back, 'dp', scatter_dimension=1, tiled=True)]
  transfers between devices with their start and end apart: 14 -> 12, of which waited for: 6 -> 6; matrix products, arithmetic and copies ran while one was open for 32% -> 24% of each run, Pallas kernels for 0% -> 0%
where the time goes in v5:
time: 546 us; the launch traced here: 536 us
  blocking collectives  174 us (32%)
  waiting for transfers between devices  109 us (20%)
  matrix products  91.4 us (17%)
  local copies, waits for them, and re-layouts  74 us (14%)
  other arithmetic  37.7 us (7%)
  starting transfers between devices  34 us (6%)
  between operations  14.8 us (3%)
    all_to_all x2, blocking collectives, spread_quarter(): lax.all_to_all(copies, 'mp', split_axis=0, concat_axis=0, tiled=True)  96.3 us
    all_to_all x2, waiting for transfers between devices, gather_quarter_exchange(): lax.all_to_all(pieces, 'mp', split_axis=0, concat_axis=0, tiled=True)  85.6 us
    dot_general x16, matrix products, blockwise_grad(): jnp.dot(left[:, block * rows:(block + 1) * rows], right[block * rows:(blo...  44.6 us
    all_gather x1, blocking collectives, shards(): lax.all_gather(jnp.stack([block_mean, block_m2]), 'mp', axis=0, tiled=False)  22.2 us
    psum x1, blocking collectives, shards(): lax.psum((jnp.sum(scaled, axis=1), jnp.sum(scaled * normed, axis=1)), 'mp')  18.8 us
    all_to_all x1, blocking collectives, shards(): lax.all_to_all(projected, 'mp', split_axis=2, concat_axis=1, tiled=True)  15 us
    ppermute x4, starting transfers between devices, swap(): return lax.ppermute(block, ('dp', 'mp'), swap_pairs(n_dp, n_mp))  13.3 us
    reshape x4, local copies, waits for them, and re-layouts, gather_quarter_exchange(): pieces = partial.reshape(n_dp, rows, ratio, width)  11.7 us
  transfers between devices with their start and end apart: 12, of which 6 were waited for; matrix products, arithmetic and copies ran while one was open for 24% of the time, Pallas kernels for 0%

profile of v5, /device:TPU:0, one launch (start us, length us, event | category | flops | bytes accessed | tf_op | source)
XLA Modules:
  0.0 535.6 jit_solution(2212111605436573368)
XLA Ops:
  10.3 22.2 %all-gather.1 = f32[8,2,128]{2,1,0:T(2,128)S(1)} all-gather(f32[1,2,128]{2,1,0:T(2,128)S(1)} %maximum_bitcast_fusion), channel_id=2, replica_groups=mesh['dp'=4,'mp'=8] {'mp'}, dimensions={0}, use_global_device_ids=true | all-gather | bytes 9216 | tf_op jit(solution)/shard_map/all_gather | solution.py:181
  37.9 47.8 %all_to_all.80 = bf16[8,128,768]{1,2,0:T(8,128)(2,1)} all-to-all(bf16[8,128,768]{1,2,0:T(8,128)(2,1)S(1)} %broadcast_in_dim.7), channel_id=1, replica_groups=mesh['dp'=4,'mp'=8] {'mp'}, dimensions={0} | all-to-all | bytes 3145728 | tf_op jit(solution)/shard_map/all_to_all | solution.py:131
  85.7 4.9 copy.68
  94.7 2.6 convolution_bitcast_fusion.1
  97.4 2.7 pad_maximum_fusion
  100.2 3.0 collective-permute-start
  106.1 48.5 %all_to_all.81 = bf16[8,128,768]{1,2,0:T(8,128)(2,1)} all-to-all(bf16[8,128,768]{1,2,0:T(8,128)(2,1)S(1)} %broadcast_in_dim.6), channel_id=1, replica_groups=mesh['dp'=4,'mp'=8] {'mp'}, dimensions={0} | all-to-all | bytes 3145728 | tf_op jit(solution)/shard_map/all_to_all | solution.py:131
  154.6 4.9 copy.66
  159.5 2.8 copy.91
  162.4 2.9 convolution_bitcast_fusion.3
  165.2 4.6 convolution_bitcast_fusion
  176.7 15.0 %all_to_all.82 = bf16[3,16,24,128]{3,1,0,2:T(8,128)(2,1)S(1)} all-to-all(bf16[3,16,24,128]{3,1,0,2:T(8,128)(2,1)S(1)} %copy.70), channel_id=1, replica_groups=mesh['dp'=4,'mp'=8] {'mp'}, dimensions={2} | all-to-all | bytes 589824 | tf_op jit(solution)/shard_map/all_to_all | solution.py:210
  197.9 2.6 copy.74
  200.4 2.5 reshape.209
  207.1 6.9 %reduce-scatter.5.cloned.1.call-done = f32[1920,128]{0,1:T(8,128)} async-done(((f32[1920,512]{0,1:T(8,128)}), f32[1920,128]{0,1:T(8,128)}) %reduce-scatter.5.cloned.1.call-update) | async-done | bytes 983056 | tf_op jit(solution)/shard_map/reduce_scatter | solution.py:251
  218.8 5.7 %all-to-all-start.5 = ((bf16[16,24,128]{2,0,1:T(8,128)(2,1)}), bf16[16,24,128]{2,0,1:T(8,128)(2,1)}, u32[]{:S(2)}, u32[]{:S(2)}) async-start(bf16[16,24,128]{2,0,1:T(8,128)(2,1)} %copy.82), calls=%async_computation.7 | async-start | bytes 196608 | tf_op jit(solution)/shard_map/all_to_all | solution.py:255
  226.4 5.3 all-to-all-done.5
  240.8 3.3 fusion.102
  244.1 4.2 bitcast_reduce_fusion
  256.8 4.1 all-to-all-start.6
  261.0 2.6 fusion.44
  263.6 8.0 %all-to-all-done.6 = bf16[3,128,3,128]{3,2,0,1:T(4,128)(2,1)} async-done(((bf16[3,128,3,128]{3,2,0,1:T(4,128)(2,1)}), bf16[3,128,3,128]{3,2,0,1:T(4,128)(2,1)}, u32[]{:S(2)}, u32[]{:S(2)}) %all-to-all-start.6) | async-done | bytes 294944 | tf_op jit(solution)/shard_map/all_to_all | solution.py:265
  283.6 11.0 %all_to_all.83 = bf16[128,3,128]{2,1,0:T(4,128)(2,1)S(1)} all-to-all(bf16[128,3,128]{2,1,0:T(4,128)(2,1)} %copy.75), channel_id=1, replica_groups=mesh['dp'=4,'mp'=8] {'mp'}, dimensions={0} | all-to-all | bytes 196608 | tf_op jit(solution)/shard_map/all_to_all | solution.py:217
  300.5 3.5 all-gather.7.cloned.1.call-done
  304.0 3.6 fusion.31
  307.6 6.7 %convolution_add_fusion.1 = f32[512,1536]{1,0:T(8,128)} fusion(f32[512,1536]{1,0:T(8,128)S(1)} %fusion.31, bf16[1536,1536]{1,0:T(8,128)(2,1)} %param.11, bf16[2688,512]{0,1:T(8,128)(2,1)S(1)} %copy-done.7), kind=kOutput, calls=%fused_computation.29 | convolution fusion | flops 2416705536 | bytes 12582912 | tf_op jit(solution)/shard_map/dot_general | solution.py:287
  314.3 3.8 reshape.205
  320.1 5.9 %all-to-all-start.7 = ((f32[8,128,768]{2,1,0:T(8,128)}), f32[8,128,768]{2,1,0:T(8,128)}, u32[]{:S(2)}, u32[]{:S(2)}) async-start(f32[8,128,768]{2,1,0:T(8,128)} %bitcast.170), calls=%async_computation.9 | async-start | bytes 6291456 | tf_op jit(solution)/shard_map/all_to_all | solution.py:152
  329.1 5.0 fusion.29
  334.2 3.6 convolution_add_fusion
  337.8 3.8 reshape.200
  346.7 3.6 convolution_convert_fusion.5
  350.3 3.6 convolution_convert_fusion.4
  353.9 3.5 convolution_convert_fusion.6
  357.5 39.7 %all-to-all-done.7 = f32[8,128,768]{2,1,0:T(8,128)} async-done(((f32[8,128,768]{2,1,0:T(8,128)}), f32[8,128,768]{2,1,0:T(8,128)}, u32[]{:S(2)}, u32[]{:S(2)}) %all-to-all-start.7) | async-done | bytes 3145760 | tf_op jit(solution)/shard_map/all_to_all | solution.py:152
  397.2 4.9 all-to-all-start.4
  403.6 3.4 fusion.13
  407.1 5.8 %add_convert_fusion = bf16[1536,1536]{1,0:T(8,128)(2,1)} fusion(bf16[1536,1536]{1,0:T(8,128)(2,1)S(1)} %copy-done.2, bf16[1536,1536]{1,0:T(8,128)(2,1)S(1)} %bitcast.157, bf16[1536,1536]{1,0:T(8,128)(2,1)} %convolution_convert_fusion.6, bf16[128,1536]{0,1:T(8,128)(2,1)S(1)} %bitcast.188, bf16[1920,512]{0,1:T(8,128)(2,1)} %all-gather.5.cloned.1.call-done), kind=kOutput, calls=%fused_computation.1 | convolution fusion | flops 625213440 | bytes 19660800 | tf_op jit(solution)/shard_map/dot_general | solution.py:160
  419.4 4.0 fusion.5
  423.5 3.9 add_convert_fusion.1
  427.4 2.8 reduce_sum.209
  430.2 4.5 collective-permute-start.3
  434.7 6.3 %fusion.3 = bf16[1152,1536]{1,0:T(8,128)(2,1)} fusion(f32[1152,1536]{1,0:T(8,128)} %fusion.5, bf16[128,1536]{0,1:T(8,128)(2,1)} %bitcast.174, bf16[2688,512]{0,1:T(8,128)(2,1)} %all-gather.7.cloned.1.call-done), kind=kOutput, calls=%fused_computation.6 | convolution fusion | flops 460062720 | bytes 11304960 | tf_op jit(solution)/shard_map/dot_general | solution.py:160
  441.0 45.8 %all-to-all-done.4 = f32[8,128,768]{2,1,0:T(8,128)} async-done(((f32[8,128,768]{2,1,0:T(8,128)}), f32[8,128,768]{2,1,0:T(8,128)}, u32[]{:S(2)}, u32[]{:S(2)}) %all-to-all-start.4) | async-done | bytes 3145760 | tf_op jit(solution)/shard_map/all_to_all | solution.py:152
  486.8 2.9 reduce_sum.202
  489.7 4.5 collective-permute-start.2
  496.0 10.9 %psum.23 = f32[768]{0:T(1024)} all-reduce(f32[768]{0:T(1024)S(1)} %get-tuple-element.13), channel_id=1, replica_groups=mesh['dp'=4,'mp'=8] {'dp'}, use_global_device_ids=true, to_apply=%region_25.0 | all-reduce | flops 768 | bytes 6144 | tf_op jit(solution)/shard_map/psum | solution.py:299
  506.8 18.8 %all-reduce = (f32[128]{0:T(128)}, f32[128]{0:T(128)S(1)}) all-reduce(f32[128]{0:T(128)} %get-tuple-element.14, f32[128]{0:T(128)} %get-tuple-element.15), channel_id=1, replica_groups=mesh['dp'=4,'mp'=8] {'mp'}, use_global_device_ids=true, to_apply=%region_23.0 | all-reduce | flops 256 | bytes 2048 | tf_op jit(solution)/shard_map/psum | solution.py:291
  (167 shorter events, 97.7 us)
Async XLA Ops:
  7.2 85.3 %copy-start = (bf16[3,16,24,1536]{3,2,1,0:T(8,128)(2,1)S(1)}, bf16[3,16,24,1536]{3,2,1,0:T(8,128)(2,1)}, u32[]{:S(2)}) copy-start(bf16[3,16,24,1536]{3,2,1,0:T(8,128)(2,1)} %param.9) | copy-start | bytes 10616836
  7.2 155.2 %reduce-scatter.3.cloned.1.call-start = ((), (), s32[]{:S(2)}) async-start(), calls=%async_computation.10 | async-start | bytes 6881280 | tf_op jit(solution)/shard_map/reduce_scatter | solution.py:200
  32.5 2.5 copy-start.26
  32.6 2.4 copy-start.28
  33.7 1.3 collective-permute-start.1
  90.6 4.1 slice-start.2
  92.5 2.3 slice-start.3
  100.1 113.9 %reduce-scatter.5.cloned.1.call-start = ((), (), s32[]{:S(2)}) async-start(), calls=%async_computation.12 | async-start | bytes 4915200 | tf_op jit(solution)/shard_map/reduce_scatter | solution.py:251
  100.2 3.0 collective-permute-start
  162.3 2.9 copy-start.19
  191.8 0.7 copy-start.18
  202.9 3.1 copy-start.21
  202.9 3.1 copy-start.24
  202.9 3.1 copy-start.25
  204.3 1.1 copy-start.5
  205.5 0.6 copy-start.23
  218.8 12.9 %all-to-all-start.5 = ((bf16[16,24,128]{2,0,1:T(8,128)(2,1)}), bf16[16,24,128]{2,0,1:T(8,128)(2,1)}, u32[]{:S(2)}, u32[]{:S(2)}) async-start(bf16[16,24,128]{2,0,1:T(8,128)(2,1)} %copy.82), calls=%async_computation.7 | async-start | bytes 196608 | tf_op jit(solution)/shard_map/all_to_all | solution.py:255
  252.5 2.9 copy-start.17
  252.6 3.2 copy-start.22
  256.8 14.7 %all-to-all-start.6 = ((bf16[3,128,3,128]{3,2,0,1:T(4,128)(2,1)}), bf16[3,128,3,128]{3,2,0,1:T(4,128)(2,1)}, u32[]{:S(2)}, u32[]{:S(2)}) async-start(bf16[3,128,3,128]{3,2,0,1:T(4,128)(2,1)} %copy.85), calls=%async_computation.8 | async-start | bytes 786432 | tf_op jit(solution)/shard_map/all_to_all | solution.py:265
  260.9 43.1 %all-gather.7.cloned.1.call-start = ((), (), s32[]{:S(2)}) async-start(), calls=%async_computation.13 | async-start | bytes 3440640 | tf_op jit(solution)/shard_map/all_gather | solution.py:279
  279.4 49.7 %all-gather.5.cloned.1.call-start = ((), (), s32[]{:S(2)}) async-start(), calls=%async_computation.11 | async-start | bytes 2457600 | tf_op jit(solution)/shard_map/all_gather | solution.py:232
  304.0 3.6 copy-start.7
  320.1 5.9 %copy-start.3 = (bf16[8,128,768]{1,2,0:T(8,128)(2,1)S(1)}, bf16[8,128,768]{1,2,0:T(8,128)(2,1)}, u32[]{:S(2)}) copy-start(bf16[8,128,768]{1,2,0:T(8,128)(2,1)} %all_to_all.80) | copy-start | bytes 4718596
  320.1 77.1 %all-to-all-start.7 = ((f32[8,128,768]{2,1,0:T(8,128)}), f32[8,128,768]{2,1,0:T(8,128)}, u32[]{:S(2)}, u32[]{:S(2)}) async-start(f32[8,128,768]{2,1,0:T(8,128)} %bitcast.170), calls=%async_computation.9 | async-start | bytes 6291456 | tf_op jit(solution)/shard_map/all_to_all | solution.py:152
  326.0 1.9 copy-start.4
  327.9 85.0 %copy-start.9 = (bf16[1,128,2,768]{1,3,2,0:T(8,128)(2,1)}, bf16[1,128,2,768]{1,3,2,0:T(8,128)(2,1)S(1)}, u32[]{:S(2)}) copy-start(bf16[1,128,2,768]{1,3,2,0:T(8,128)(2,1)S(1)} %get-tuple-element.26) | copy-start | bytes 1179652
  329.1 5.0 copy-start.20
  341.7 2.2 copy-start.6
  341.7 2.5 copy-start.11
  343.7 1.1 copy-start.12
  350.3 3.6 copy-start.10
  397.2 6.4 %copy-start.16 = (bf16[1,128,2,768]{1,3,2,0:T(8,128)(2,1)S(1)}, bf16[1,128,2,768]{1,3,2,0:T(8,128)(2,1)}, u32[]{:S(2)}) copy-start(bf16[1,128,2,768]{1,3,2,0:T(8,128)(2,1)} %get-tuple-element.22) | copy-start | bytes 1179652
  397.2 89.6 %all-to-all-start.4 = ((f32[8,128,768]{2,1,0:T(8,128)}), f32[8,128,768]{2,1,0:T(8,128)}, u32[]{:S(2)}, u32[]{:S(2)}) async-start(f32[8,128,768]{2,1,0:T(8,128)} %bitcast.26), calls=%async_computation.5 | async-start | bytes 6291456 | tf_op jit(solution)/shard_map/all_to_all | solution.py:152
  402.0 5.0 copy-start.2
  403.6 3.5 slice-start
  403.6 3.5 slice-start.1
  407.1 5.8 %copy-start.8 = (bf16[2688,512]{0,1:T(8,128)(2,1)S(1)}, bf16[2688,512]{0,1:T(8,128)(2,1)}, u32[]{:S(2)}) copy-start(bf16[2688,512]{0,1:T(8,128)(2,1)} %all-gather.7.cloned.1.call-done) | copy-start | bytes 8257540
  412.9 1.4 copy-start.14
  414.3 1.4 copy-start.15
  415.8 1.4 copy-start.13
  430.2 63.9 %collective-permute-start.3 = (f32[128,768]{1,0:T(8,128)}, f32[128,768]{1,0:T(8,128)}, u32[]{:S(2)}, u32[]{:S(2)}) collective-permute-start(f32[128,768]{1,0:T(8,128)} %reduce_sum.209), channel_id=1, source_target_pairs={{0,0},{1,1},{2,8},{3,9},{4,16},{5,17},{6,24},{7,25},{8,2},{9,3},{1... | collective-permute-start | bytes 1179656 | tf_op jit(solution)/shard_map/ppermute | solution.py:123
  434.7 93.9 %copy-start.1 = (bf16[3,16,24,1536]{3,2,1,0:T(8,128)(2,1)S(1)}, bf16[3,16,24,1536]{3,2,1,0:T(8,128)(2,1)}, u32[]{:S(2)}) copy-start(bf16[3,16,24,1536]{3,2,1,0:T(8,128)(2,1)} %param.9) | copy-start | bytes 10616836
  441.0 53.2 %copy-start.27 = (f32[128]{0:T(128)S(1)}, f32[128]{0:T(128)}, u32[]{:S(2)}) copy-start(f32[128]{0:T(128)} %copy-done.26) | copy-start | bytes 1540
  441.0 53.2 %copy-start.29 = (f32[128]{0:T(128)S(1)}, f32[128]{0:T(128)}, u32[]{:S(2)}) copy-start(f32[128]{0:T(128)} %copy-done.28) | copy-start | bytes 1540
  489.7 36.7 %collective-permute-start.2 = (f32[128,768]{1,0:T(8,128)}, f32[128,768]{1,0:T(8,128)}, u32[]{:S(2)}, u32[]{:S(2)}) collective-permute-start(f32[128,768]{1,0:T(8,128)} %reduce_sum.202), channel_id=1, source_target_pairs={{0,0},{1,1},{2,8},{3,9},{4,16},{5,17},{6,24},{7,25},{8,2},{9,3},{1... | collective-permute-start | bytes 1179656 | tf_op jit(solution)/shard_map/ppermute | solution.py:123
Sparse Core Ops, SparseCore 0:
  100.2 51.3 reduce-scatter.2
  172.1 41.8 reduce-scatter.4
  279.5 24.4 all-gather.6
  306.0 21.8 all-gather.4
